TPU v7x, 128 devices: a whole 4x4x4 slice. The times are simulated.
128 devices in a mesh: head: 4 (over x), ctx: 8 (over y, z_hi), inner: 4 (over z_lo, core).
Axes of the slice: x: 4, y: 4, z: 4 (z_hi: 2, z_lo: 2; z = z_hi * 2 + z_lo), core: 2. Of those that a mesh axis runs over, the one named last changes fastest.
Arguments:
- query_rows: bfloat16 [16384, 48, 128], P(('head', 'ctx', 'inner')), may hold values from -6 to 6
- key_rows: bfloat16 [16384, 48, 128], P(('head', 'ctx', 'inner')), may hold values from -6 to 6
- value_rows: bfloat16 [16384, 48, 128], P(('head', 'ctx', 'inner')), may hold values from -6 to 6
- grad_rows: bfloat16 [16384, 48, 128], P(('head', 'ctx', 'inner')), may hold values from -6 to 6
Outputs:
- grad_query: bfloat16 [16384, 48, 128], P(('head', 'ctx', 'inner'))
- grad_key: bfloat16 [16384, 48, 128], P(('head', 'ctx', 'inner'))
- grad_value: bfloat16 [16384, 48, 128], P(('head', 'ctx', 'inner'))
All inputs are finite; a program needn't handle non-finite values.
Results may differ from a plain program's by a relative error of at most 0.012.
The roundings to bfloat16 on the way count: a program that leaves them out, or rounds other values in their place, can miss the bound.
Values may be sent and summed in bfloat16 or wider, within the bound.
No kernel may reach another device: no remote copies, remote signals or barrier semaphores. Data moves between devices by JAX's collectives and lax.ppermute only.
A program may use at most 128 MiB of HBM per device.

v0:
```python
import jax
import jax.numpy as jnp
from jax import lax
from jax.sharding import PartitionSpec as P

CHUNKS = 4
ALL_AXES = ("head", "ctx", "inner")


def tile_scores(query_block, key_block, score_scale):
    return (
        jnp.einsum("ihd,jhd->hij", query_block, key_block, preferred_element_type=jnp.float32)
        * score_scale
    )


def tile_sight(row_count, prev_valid):
    rows_iota = lax.broadcasted_iota(jnp.int32, (row_count, row_count), 0)
    cols_iota = lax.broadcasted_iota(jnp.int32, (row_count, row_count), 1)
    return ((cols_iota > rows_iota) & prev_valid, cols_iota <= rows_iota)


def block_side(query_block, grad_block, key_prev, value_prev, key_own, value_own, prev_valid):
    score_scale = query_block.shape[-1] ** (-0.5)
    sees_prev, sees_own = tile_sight(query_block.shape[0], prev_valid)
    scores_prev = tile_scores(query_block, key_prev, score_scale)
    scores_own = tile_scores(query_block, key_own, score_scale)
    row_top = jnp.maximum(
        jnp.max(jnp.where(sees_prev, scores_prev, -jnp.inf), axis=-1),
        jnp.max(jnp.where(sees_own, scores_own, -jnp.inf), axis=-1),
    )
    row_total = jnp.sum(
        jnp.where(sees_prev, jnp.exp(scores_prev - row_top[..., None]), 0.0), axis=-1
    )
    row_total = row_total + jnp.sum(
        jnp.where(sees_own, jnp.exp(scores_own - row_top[..., None]), 0.0), axis=-1
    )
    log_total = row_top + jnp.log(row_total)
    prob_prev = jnp.where(sees_prev, jnp.exp(scores_prev - log_total[..., None]), 0.0)
    prob_own = jnp.where(sees_own, jnp.exp(scores_own - log_total[..., None]), 0.0)
    prob_prev_b = prob_prev.astype(jnp.bfloat16)
    prob_own_b = prob_own.astype(jnp.bfloat16)
    attended = jnp.einsum(
        "hij,jhd->ihd", prob_prev_b, value_prev, preferred_element_type=jnp.float32
    )
    attended = attended + jnp.einsum(
        "hij,jhd->ihd", prob_own_b, value_own, preferred_element_type=jnp.float32
    )
    row_delta = jnp.sum(grad_block.astype(jnp.float32) * attended, axis=-1).T
    dprob_prev = jnp.einsum(
        "ihd,jhd->hij", grad_block, value_prev, preferred_element_type=jnp.float32
    )
    dprob_own = jnp.einsum(
        "ihd,jhd->hij", grad_block, value_own, preferred_element_type=jnp.float32
    )
    dscore_prev = (prob_prev * (dprob_prev - row_delta[..., None])).astype(jnp.bfloat16)
    dscore_own = (prob_own * (dprob_own - row_delta[..., None])).astype(jnp.bfloat16)
    grad_q = jnp.einsum("hij,jhd->ihd", dscore_prev, key_prev, preferred_element_type=jnp.float32)
    grad_q = (
        grad_q + jnp.einsum("hij,jhd->ihd", dscore_own, key_own, preferred_element_type=jnp.float32)
    ) * score_scale
    grad_k_own = (
        jnp.einsum("hij,ihd->jhd", dscore_own, query_block, preferred_element_type=jnp.float32)
        * score_scale
    )
    grad_v_own = jnp.einsum(
        "hij,ihd->jhd", prob_own_b, grad_block, preferred_element_type=jnp.float32
    )
    grad_k_prev = (
        jnp.einsum("hij,ihd->jhd", dscore_prev, query_block, preferred_element_type=jnp.float32)
        * score_scale
    )
    grad_v_prev = jnp.einsum(
        "hij,ihd->jhd", prob_prev_b, grad_block, preferred_element_type=jnp.float32
    )
    return grad_q, grad_k_own, grad_v_own, grad_k_prev, grad_v_prev


def halo_pairs(heads, cycle):
    pairs = []
    for h in range(heads):
        for c in range(cycle):
            src = h * cycle + c
            if h < heads // 2:
                if c + 1 < cycle:
                    pairs.append((src, src + 1))
                else:
                    pairs.append((src, (heads - 1 - h) * cycle + c))
            elif c > 0:
                pairs.append((src, src - 1))
    return pairs


def on_device(query_rows, key_rows, value_rows, grad_rows):
    heads = lax.axis_size("head")
    cycle = lax.axis_size(("ctx", "inner"))
    h = lax.axis_index("head")
    c = lax.axis_index(("ctx", "inner"))
    keep_low = (h == 1) | (h == 2)
    is_first = h % 2 == 0
    prev_valid = (h >= heads // 2) | (c > 0)
    partner = [(i, i ^ 1) for i in range(heads)]
    forward = halo_pairs(heads, cycle)
    backward = [(t, s) for s, t in forward]

    rows, all_heads, hd = query_rows.shape
    half = all_heads // 2
    hc = half // CHUNKS
    stacked = jnp.stack([query_rows, key_rows, value_rows, grad_rows])
    split = stacked.reshape(4, rows, 2, CHUNKS, hc, hd)
    keep = jnp.where(keep_low, split[:, :, 0], split[:, :, 1])
    send = jnp.where(keep_low, split[:, :, 1], split[:, :, 0])

    own_parts, back_parts = [], []
    for i in range(CHUNKS):
        own_i = keep[:, :, i]
        recv_i = lax.ppermute(send[:, :, i], "head", partner)
        first = jnp.where(is_first, own_i, recv_i)
        second = jnp.where(is_first, recv_i, own_i)
        blk = jnp.concatenate([first, second], axis=1)
        kv_prev = lax.ppermute(blk[1:3], ALL_AXES, forward)
        dq, dk_own, dv_own, dk_prev, dv_prev = block_side(
            blk[0], blk[3], kv_prev[0], kv_prev[1], blk[1], blk[2], prev_valid
        )
        dkv_next = lax.ppermute(
            jnp.stack([dk_prev, dv_prev]).astype(jnp.bfloat16), ALL_AXES, backward
        )
        dk = dk_own + dkv_next[0].astype(jnp.float32)
        dv = dv_own + dkv_next[1].astype(jnp.float32)
        grads = jnp.stack([dq, dk, dv]).astype(jnp.bfloat16)
        mine = jnp.where(is_first, grads[:, :rows], grads[:, rows:])
        theirs = jnp.where(is_first, grads[:, rows:], grads[:, :rows])
        own_parts.append(mine)
        back_parts.append(lax.ppermute(theirs, "head", partner))
    own_all = jnp.stack(own_parts, axis=2)
    back_all = jnp.stack(back_parts, axis=2)
    low = jnp.where(keep_low, own_all, back_all)
    high = jnp.where(keep_low, back_all, own_all)
    out = jnp.stack([low, high], axis=2).reshape(3, rows, all_heads, hd)
    return out[0], out[1], out[2]


def solution(mesh):
    spec = P(("head", "ctx", "inner"), None, None)
    return jax.shard_map(
        on_device, mesh=mesh, in_specs=(spec,) * 4, out_specs=(spec,) * 3, check_vma=False
    )
```

profile of v0, /device:TPU:24, one launch (start us, length us, event | category | flops | bytes accessed | tf_op | source)
XLA Modules:
  0.0 219.1 jit_solution(10897521737340015016)
XLA Ops:
  0.7 1.9 copy.7
  3.0 1.0 copy-done.1
  4.0 1.6 copy.9
  5.6 1.6 copy.10
  7.1 3.0 %pad_maximum_fusion = bf16[4,128,2,4,6,128]{5,1,4,0,3,2:T(8,128)(2,1)S(1)} fusion(bf16[1,128,2,4,6,128]{5,1,4,0,3,2:T(8,128)(2,1)} %bitcast.389, bf16[1,128,2,4,6,128]{5,1,4,0,3,2:T(8,128)(2,1)} %bitcast.388, bf16[1,128,2,4,6,128]{5,1,4,0,3,2:T(8,128)(2,1)S(1)} %bitcast.387, bf16[1,128,2,4,6,128]{5,1,4,0,3,2:T(8,128)(2,1)S(1)} %bitcast.386), kind=kLoop, calls=%fused_computation | loop fusion | flops 9437184 | bytes 12582912 | tf_op jit(solution)/shard_map/stack | solution.py:109
  10.6 1.7 slice_bitcast_fusion.2
  12.3 1.5 collective-permute-start
  13.8 0.5 collective-permute-start.3
  14.3 1.5 collective-permute-start.6
  15.8 0.5 collective-permute-start.9
  16.4 16.6 %collective-permute-done = bf16[4,128,6,128]{3,1,2,0:T(8,128)(2,1)} collective-permute-done((bf16[4,128,6,128]{3,1,2,0:T(8,128)(2,1)}, bf16[4,128,6,128]{3,1,2,0:T(8,128)(2,1)}, u32[]{:S(2)}, u32[]{:S(2)}) %collective-permute-start) | collective-permute-done | bytes 786464 | tf_op jit(solution)/shard_map/ppermute | solution.py:117
  33.0 16.9 %collective-permute-done.3 = bf16[4,128,6,128]{3,1,2,0:T(8,128)(2,1)} collective-permute-done((bf16[4,128,6,128]{3,1,2,0:T(8,128)(2,1)}, bf16[4,128,6,128]{3,1,2,0:T(8,128)(2,1)}, u32[]{:S(2)}, u32[]{:S(2)}) %collective-permute-start.3) | collective-permute-done | bytes 786464 | tf_op jit(solution)/shard_map/ppermute | solution.py:117
  49.9 16.9 %collective-permute-done.6 = bf16[4,128,6,128]{3,1,2,0:T(8,128)(2,1)} collective-permute-done((bf16[4,128,6,128]{3,1,2,0:T(8,128)(2,1)}, bf16[4,128,6,128]{3,1,2,0:T(8,128)(2,1)}, u32[]{:S(2)}, u32[]{:S(2)}) %collective-permute-start.6) | collective-permute-done | bytes 786464 | tf_op jit(solution)/shard_map/ppermute | solution.py:117
  66.8 15.7 %collective-permute-done.9 = bf16[4,128,6,128]{3,1,2,0:T(8,128)(2,1)} collective-permute-done((bf16[4,128,6,128]{3,1,2,0:T(8,128)(2,1)}, bf16[4,128,6,128]{3,1,2,0:T(8,128)(2,1)}, u32[]{:S(2)}, u32[]{:S(2)}) %collective-permute-start.9) | collective-permute-done | bytes 786464 | tf_op jit(solution)/shard_map/ppermute | solution.py:117
  82.5 2.3 %broadcast_select_fusion.4 = (bf16[4,128,6,128]{3,1,2,0:T(8,128)(2,1)S(1)}, bf16[4,128,6,128]{3,1,2,0:T(8,128)(2,1)S(1)}, bf16[4,128,6,128]{3,1,2,0:T(8,128)(2,1...) fusion(bf16[4,128,6,128]{3,1,2,0:T(8,128)(2,1)} %collective-per, ...), kind=kLoop, calls=%fused_computation.200 | loop fusion | flops 3145728 | bytes 12582913 | tf_op jit(solution)/shard_map/jit(_where)/select_n | solution.py:119
  85.5 1.9 collective-permute-start.4
  87.4 3.9 %collective-permute-start.7 = (bf16[2,256,6,128]{3,1,2,0:T(8,128)(2,1)S(1)}, bf16[2,256,6,128]{3,1,2,0:T(8,128)(2,1)S(1)}, u32[]{:S(2)}, u32[]{:S(2)}) collective-permute-start(bf16[2,256,6,128]{3,1,2,0:T(8,128)(2,1)S(1)} %fusion.67), channel_id=1, source_target_pairs={{0,1},{1,2},{2,3},{3,4},{4,5},{5,6},{6,7},{7,8},{8,9},{9,10},{10,1... | collective-permute-start | bytes 2359304 | tf_op jit(solution)/shard_map/ppermute | solution.py:121
  91.3 1.9 collective-permute-start.1
  93.2 4.1 %collective-permute-start.10 = (bf16[2,256,6,128]{3,1,2,0:T(8,128)(2,1)S(1)}, bf16[2,256,6,128]{3,1,2,0:T(8,128)(2,1)S(1)}, u32[]{:S(2)}, u32[]{:S(2)}) collective-permute-start(bf16[2,256,6,128]{3,1,2,0:T(8,128)(2,1)S(1)} %fusion.66), channel_id=1, source_target_pairs={{0,1},{1,2},{2,3},{3,4},{4,5},{5,6},{6,7},{7,8},{8,9},{9,10},{10,1... | collective-permute-start | bytes 2359304 | tf_op jit(solution)/shard_map/ppermute | solution.py:121
  98.5 19.2 %collective-permute-done.1 = bf16[2,256,6,128]{3,1,2,0:T(8,128)(2,1)S(1)} collective-permute-done((bf16[2,256,6,128]{3,1,2,0:T(8,128)(2,1)S(1)}, bf16[2,256,6,128]{3,1,2,0:T(8,128)(2,1)S(1)}, u32[]{:S(2)}, u32[]{:S(2)}) %collective-permute-start.1) | collective-permute-done | bytes 786464 | tf_op jit(solution)/shard_map/ppermute | solution.py:121
  118.5 7.6 %collective-permute-done.10 = bf16[2,256,6,128]{3,1,2,0:T(8,128)(2,1)S(1)} collective-permute-done((bf16[2,256,6,128]{3,1,2,0:T(8,128)(2,1)S(1)}, bf16[2,256,6,128]{3,1,2,0:T(8,128)(2,1)S(1)}, u32[]{:S(2)}, u32[]{:S(2)}) %collective-permute-start.10) | collective-permute-done | bytes 786464 | tf_op jit(solution)/shard_map/ppermute | solution.py:121
  126.9 1.7 select_reduce_fusion.12
  129.7 0.7 multiply_reduce_fusion.3
  132.2 1.9 collective-permute-start.2
  134.2 1.8 select_reduce_fusion.9
  135.9 0.5 fusion.110
  137.0 0.7 multiply_reduce_fusion.2
  139.5 4.3 %collective-permute-start.5 = (bf16[2,256,6,128]{1,3,2,0:T(8,128)(2,1)S(1)}, bf16[2,256,6,128]{1,3,2,0:T(8,128)(2,1)S(1)}, u32[]{:S(2)}, u32[]{:S(2)}) collective-permute-start(bf16[2,256,6,128]{1,3,2,0:T(8,128)(2,1)S(1)} %pad_maximum_fusion.9), channel_id=1, source_target_pairs={{1,0},{2,1},{3,2},{4,3},{5,4},{6,5},{7,6},{8,7},{9,8},{10,9},{11,1... | collective-permute-start | bytes 2359304 | tf_op jit(solution)/shard_map/ppermute | solution.py:125
  143.8 0.5 fusion.105
  144.8 0.7 multiply_reduce_fusion.1
  147.3 1.9 collective-permute-start.8
  150.3 0.7 multiply_reduce_fusion
  152.0 2.4 %collective-permute-start.11 = (bf16[2,256,6,128]{1,3,2,0:T(8,128)(2,1)S(1)}, bf16[2,256,6,128]{1,3,2,0:T(8,128)(2,1)S(1)}, u32[]{:S(2)}, u32[]{:S(2)}) collective-permute-start(bf16[2,256,6,128]{1,3,2,0:T(8,128)(2,1)S(1)} %pad_maximum_fusion.11), channel_id=1, source_target_pairs={{1,0},{2,1},{3,2},{4,3},{5,4},{6,5},{7,6},{8,7},{9,8},{10,9},{11,1... | collective-permute-start | bytes 2359304 | tf_op jit(solution)/shard_map/ppermute | solution.py:125
  157.6 1.6 collective-permute-start.12
  160.3 0.6 collective-permute-start.13
  160.9 0.6 collective-permute-done.8
  162.6 1.8 collective-permute-start.14
  164.4 5.5 %collective-permute-done.11 = bf16[2,256,6,128]{1,3,2,0:T(8,128)(2,1)S(1)} collective-permute-done((bf16[2,256,6,128]{1,3,2,0:T(8,128)(2,1)S(1)}, bf16[2,256,6,128]{1,3,2,0:T(8,128)(2,1)S(1)}, u32[]{:S(2)}, u32[]{:S(2)}) %collective-permute-start.11) | collective-permute-done | bytes 786464 | tf_op jit(solution)/shard_map/ppermute | solution.py:125
  171.0 1.6 collective-permute-start.15
  172.6 1.3 collective-permute-done.12
  173.9 12.6 %collective-permute-done.13 = bf16[3,128,6,128]{1,3,2,0:T(8,128)(2,1)S(1)} collective-permute-done((bf16[3,128,6,128]{1,3,2,0:T(8,128)(2,1)S(1)}, bf16[3,128,6,128]{1,3,2,0:T(8,128)(2,1)S(1)}, u32[]{:S(2)}, u32[]{:S(2)}) %collective-permute-start.13) | collective-permute-done | bytes 589856 | tf_op jit(solution)/shard_map/ppermute | solution.py:134
  186.5 12.6 %collective-permute-done.14 = bf16[3,128,6,128]{1,3,2,0:T(8,128)(2,1)S(1)} collective-permute-done((bf16[3,128,6,128]{1,3,2,0:T(8,128)(2,1)S(1)}, bf16[3,128,6,128]{1,3,2,0:T(8,128)(2,1)S(1)}, u32[]{:S(2)}, u32[]{:S(2)}) %collective-permute-start.14) | collective-permute-done | bytes 589856 | tf_op jit(solution)/shard_map/ppermute | solution.py:134
  199.2 11.7 %collective-permute-done.15 = bf16[3,128,6,128]{1,3,2,0:T(8,128)(2,1)S(1)} collective-permute-done((bf16[3,128,6,128]{1,3,2,0:T(8,128)(2,1)S(1)}, bf16[3,128,6,128]{1,3,2,0:T(8,128)(2,1)S(1)}, u32[]{:S(2)}, u32[]{:S(2)}) %collective-permute-start.15) | collective-permute-done | bytes 589856 | tf_op jit(solution)/shard_map/ppermute | solution.py:134
  210.8 0.7 broadcast_select_fusion
  211.5 1.4 pad_maximum_fusion.3
  212.9 2.7 %copy.91 = bf16[128,48,128]{2,1,0:T(8,128)(2,1)} copy(bf16[128,48,128]{0,2,1:T(8,128)(2,1)} %bitcast.391) | data formatting | bytes 3145728
  215.6 1.7 copy.92
  217.4 1.7 copy.93
  (79 shorter events, 20.0 us)
Async XLA Ops:
  0.6 1.9 copy-start
  2.6 1.4 copy-start.1
  4.0 1.6 copy-start.2
  12.3 20.7 %collective-permute-start = (bf16[4,128,6,128]{3,1,2,0:T(8,128)(2,1)}, bf16[4,128,6,128]{3,1,2,0:T(8,128)(2,1)}, u32[]{:S(2)}, u32[]{:S(2)}) collective-permute-start(bf16[4,128,6,128]{3,1,2,0:T(8,128)(2,1)} %get-tuple-element.51), channel_id=1, source_target_pairs={{0,32},{32,0},{64,96},{96,64},{1,33},{33,1},{65,97},{97,65},{2,34}... | collective-permute-start | bytes 2359304 | tf_op jit(solution)/shard_map/ppermute | solution.py:117
  13.8 36.1 %collective-permute-start.3 = (bf16[4,128,6,128]{3,1,2,0:T(8,128)(2,1)}, bf16[4,128,6,128]{3,1,2,0:T(8,128)(2,1)}, u32[]{:S(2)}, u32[]{:S(2)}) collective-permute-start(bf16[4,128,6,128]{3,1,2,0:T(8,128)(2,1)} %get-tuple-element.50), channel_id=1, source_target_pairs={{0,32},{32,0},{64,96},{96,64},{1,33},{33,1},{65,97},{97,65},{2,34}... | collective-permute-start | bytes 2359304 | tf_op jit(solution)/shard_map/ppermute | solution.py:117
  14.3 52.4 %collective-permute-start.6 = (bf16[4,128,6,128]{3,1,2,0:T(8,128)(2,1)}, bf16[4,128,6,128]{3,1,2,0:T(8,128)(2,1)}, u32[]{:S(2)}, u32[]{:S(2)}) collective-permute-start(bf16[4,128,6,128]{3,1,2,0:T(8,128)(2,1)} %get-tuple-element.48), channel_id=1, source_target_pairs={{0,32},{32,0},{64,96},{96,64},{1,33},{33,1},{65,97},{97,65},{2,34}... | collective-permute-start | bytes 2359304 | tf_op jit(solution)/shard_map/ppermute | solution.py:117
  15.8 66.6 %collective-permute-start.9 = (bf16[4,128,6,128]{3,1,2,0:T(8,128)(2,1)}, bf16[4,128,6,128]{3,1,2,0:T(8,128)(2,1)}, u32[]{:S(2)}, u32[]{:S(2)}) collective-permute-start(bf16[4,128,6,128]{3,1,2,0:T(8,128)(2,1)} %get-tuple-element.49), channel_id=1, source_target_pairs={{0,32},{32,0},{64,96},{96,64},{1,33},{33,1},{65,97},{97,65},{2,34}... | collective-permute-start | bytes 2359304 | tf_op jit(solution)/shard_map/ppermute | solution.py:117
  85.5 41.1 %collective-permute-start.4 = (bf16[2,256,6,128]{3,1,2,0:T(8,128)(2,1)S(1)}, bf16[2,256,6,128]{3,1,2,0:T(8,128)(2,1)S(1)}, u32[]{:S(2)}, u32[]{:S(2)}) collective-permute-start(bf16[2,256,6,128]{3,1,2,0:T(8,128)(2,1)S(1)} %fusion.68), channel_id=1, source_target_pairs={{0,1},{1,2},{2,3},{3,4},{4,5},{5,6},{6,7},{7,8},{8,9},{9,10},{10,1... | collective-permute-start | bytes 2359304 | tf_op jit(solution)/shard_map/ppermute | solution.py:121
  87.4 30.7 %collective-permute-start.7 = (bf16[2,256,6,128]{3,1,2,0:T(8,128)(2,1)S(1)}, bf16[2,256,6,128]{3,1,2,0:T(8,128)(2,1)S(1)}, u32[]{:S(2)}, u32[]{:S(2)}) collective-permute-start(bf16[2,256,6,128]{3,1,2,0:T(8,128)(2,1)S(1)} %fusion.67), channel_id=1, source_target_pairs={{0,1},{1,2},{2,3},{3,4},{4,5},{5,6},{6,7},{7,8},{8,9},{9,10},{10,1... | collective-permute-start | bytes 2359304 | tf_op jit(solution)/shard_map/ppermute | solution.py:121
  91.3 26.4 %collective-permute-start.1 = (bf16[2,256,6,128]{3,1,2,0:T(8,128)(2,1)S(1)}, bf16[2,256,6,128]{3,1,2,0:T(8,128)(2,1)S(1)}, u32[]{:S(2)}, u32[]{:S(2)}) collective-permute-start(bf16[2,256,6,128]{3,1,2,0:T(8,128)(2,1)S(1)} %fusion.69), channel_id=1, source_target_pairs={{0,1},{1,2},{2,3},{3,4},{4,5},{5,6},{6,7},{7,8},{8,9},{9,10},{10,1... | collective-permute-start | bytes 2359304 | tf_op jit(solution)/shard_map/ppermute | solution.py:121
  93.2 32.9 %collective-permute-start.10 = (bf16[2,256,6,128]{3,1,2,0:T(8,128)(2,1)S(1)}, bf16[2,256,6,128]{3,1,2,0:T(8,128)(2,1)S(1)}, u32[]{:S(2)}, u32[]{:S(2)}) collective-permute-start(bf16[2,256,6,128]{3,1,2,0:T(8,128)(2,1)S(1)} %fusion.66), channel_id=1, source_target_pairs={{0,1},{1,2},{2,3},{3,4},{4,5},{5,6},{6,7},{7,8},{8,9},{9,10},{10,1... | collective-permute-start | bytes 2359304 | tf_op jit(solution)/shard_map/ppermute | solution.py:121
  132.2 24.3 %collective-permute-start.2 = (bf16[2,256,6,128]{1,3,2,0:T(8,128)(2,1)S(1)}, bf16[2,256,6,128]{1,3,2,0:T(8,128)(2,1)S(1)}, u32[]{:S(2)}, u32[]{:S(2)}) collective-permute-start(bf16[2,256,6,128]{1,3,2,0:T(8,128)(2,1)S(1)} %pad_maximum_fusion.8), channel_id=1, source_target_pairs={{1,0},{2,1},{3,2},{4,3},{5,4},{6,5},{7,6},{8,7},{9,8},{10,9},{11,1... | collective-permute-start | bytes 2359304 | tf_op jit(solution)/shard_map/ppermute | solution.py:125
  139.5 19.7 %collective-permute-start.5 = (bf16[2,256,6,128]{1,3,2,0:T(8,128)(2,1)S(1)}, bf16[2,256,6,128]{1,3,2,0:T(8,128)(2,1)S(1)}, u32[]{:S(2)}, u32[]{:S(2)}) collective-permute-start(bf16[2,256,6,128]{1,3,2,0:T(8,128)(2,1)S(1)} %pad_maximum_fusion.9), channel_id=1, source_target_pairs={{1,0},{2,1},{3,2},{4,3},{5,4},{6,5},{7,6},{8,7},{9,8},{10,9},{11,1... | collective-permute-start | bytes 2359304 | tf_op jit(solution)/shard_map/ppermute | solution.py:125
  147.3 14.2 %collective-permute-start.8 = (bf16[2,256,6,128]{1,3,2,0:T(8,128)(2,1)S(1)}, bf16[2,256,6,128]{1,3,2,0:T(8,128)(2,1)S(1)}, u32[]{:S(2)}, u32[]{:S(2)}) collective-permute-start(bf16[2,256,6,128]{1,3,2,0:T(8,128)(2,1)S(1)} %pad_maximum_fusion.10), channel_id=1, source_target_pairs={{1,0},{2,1},{3,2},{4,3},{5,4},{6,5},{7,6},{8,7},{9,8},{10,9},{11,1... | collective-permute-start | bytes 2359304 | tf_op jit(solution)/shard_map/ppermute | solution.py:125
  152.0 18.0 %collective-permute-start.11 = (bf16[2,256,6,128]{1,3,2,0:T(8,128)(2,1)S(1)}, bf16[2,256,6,128]{1,3,2,0:T(8,128)(2,1)S(1)}, u32[]{:S(2)}, u32[]{:S(2)}) collective-permute-start(bf16[2,256,6,128]{1,3,2,0:T(8,128)(2,1)S(1)} %pad_maximum_fusion.11), channel_id=1, source_target_pairs={{1,0},{2,1},{3,2},{4,3},{5,4},{6,5},{7,6},{8,7},{9,8},{10,9},{11,1... | collective-permute-start | bytes 2359304 | tf_op jit(solution)/shard_map/ppermute | solution.py:125
  157.6 16.3 %collective-permute-start.12 = (bf16[3,128,6,128]{1,3,2,0:T(8,128)(2,1)S(1)}, bf16[3,128,6,128]{1,3,2,0:T(8,128)(2,1)S(1)}, u32[]{:S(2)}, u32[]{:S(2)}) collective-permute-start(bf16[3,128,6,128]{1,3,2,0:T(8,128)(2,1)S(1)} %get-tuple-element.65), channel_id=1, source_target_pairs={{0,32},{32,0},{64,96},{96,64},{1,33},{33,1},{65,97},{97,65},{2,34}... | collective-permute-start | bytes 1769480 | tf_op jit(solution)/shard_map/ppermute | solution.py:134
  160.3 26.2 %collective-permute-start.13 = (bf16[3,128,6,128]{1,3,2,0:T(8,128)(2,1)S(1)}, bf16[3,128,6,128]{1,3,2,0:T(8,128)(2,1)S(1)}, u32[]{:S(2)}, u32[]{:S(2)}) collective-permute-start(bf16[3,128,6,128]{1,3,2,0:T(8,128)(2,1)S(1)} %get-tuple-element.67), channel_id=1, source_target_pairs={{0,32},{32,0},{64,96},{96,64},{1,33},{33,1},{65,97},{97,65},{2,34}... | collective-permute-start | bytes 1769480 | tf_op jit(solution)/shard_map/ppermute | solution.py:134
  162.6 36.5 %collective-permute-start.14 = (bf16[3,128,6,128]{1,3,2,0:T(8,128)(2,1)S(1)}, bf16[3,128,6,128]{1,3,2,0:T(8,128)(2,1)S(1)}, u32[]{:S(2)}, u32[]{:S(2)}) collective-permute-start(bf16[3,128,6,128]{1,3,2,0:T(8,128)(2,1)S(1)} %get-tuple-element.69), channel_id=1, source_target_pairs={{0,32},{32,0},{64,96},{96,64},{1,33},{33,1},{65,97},{97,65},{2,34}... | collective-permute-start | bytes 1769480 | tf_op jit(solution)/shard_map/ppermute | solution.py:134
  171.0 39.8 %collective-permute-start.15 = (bf16[3,128,6,128]{1,3,2,0:T(8,128)(2,1)S(1)}, bf16[3,128,6,128]{1,3,2,0:T(8,128)(2,1)S(1)}, u32[]{:S(2)}, u32[]{:S(2)}) collective-permute-start(bf16[3,128,6,128]{1,3,2,0:T(8,128)(2,1)S(1)} %get-tuple-element.71), channel_id=1, source_target_pairs={{0,32},{32,0},{64,96},{96,64},{1,33},{33,1},{65,97},{97,65},{2,34}... | collective-permute-start | bytes 1769480 | tf_op jit(solution)/shard_map/ppermute | solution.py:134
where the time goes:
time: 220 us; the launch traced here: 219 us
  waiting for transfers between devices  137 us (62%)
  starting transfers between devices  32.1 us (15%)
  matrix products  22.6 us (10%)
  local copies, waits for them, and re-layouts  14.4 us (7%)
  other arithmetic  11.4 us (5%)
    ppermute x4, waiting for transfers between devices, on_device(): recv_i = lax.ppermute(send[:, :, i], 'head', partner)  66.1 us
    ppermute x4, waiting for transfers between devices, on_device(): back_parts.append(lax.ppermute(theirs, 'head', partner))  38.2 us
    ppermute x4, waiting for transfers between devices, on_device(): kv_prev = lax.ppermute(blk[1:3], ALL_AXES, forward)  26.9 us
    unnamed x13, local copies, waits for them, and re-layouts  12.6 us
    ppermute x4, starting transfers between devices, on_device(): kv_prev = lax.ppermute(blk[1:3], ALL_AXES, forward)  11.9 us
    ppermute x4, starting transfers between devices, on_device(): lax.ppermute(jnp.stack([dk_prev, dv_prev]).astype(jnp.bfloat16), ALL_AXES...  10.6 us
    ppermute x4, waiting for transfers between devices, on_device(): lax.ppermute(jnp.stack([dk_prev, dv_prev]).astype(jnp.bfloat16), ALL_AXES...  6.07 us
    ppermute x4, starting transfers between devices, on_device(): back_parts.append(lax.ppermute(theirs, 'head', partner))  5.58 us
  transfers between devices with their start and end apart: 16, of which 12 were waited for; matrix products, arithmetic and copies ran while one was open for 9% of the time, Pallas kernels for 0%

commit v1 on v0

--- a/solution.py
+++ b/solution.py
@@ -106,25 +106,33 @@
     rows, all_heads, hd = query_rows.shape
     half = all_heads // 2
     hc = half // CHUNKS
-    stacked = jnp.stack([query_rows, key_rows, value_rows, grad_rows])
-    split = stacked.reshape(4, rows, 2, CHUNKS, hc, hd)
-    keep = jnp.where(keep_low, split[:, :, 0], split[:, :, 1])
-    send = jnp.where(keep_low, split[:, :, 1], split[:, :, 0])
+    inputs = (query_rows, key_rows, value_rows, grad_rows)
 
+    def chunk_of(low, i):
+        lo = jnp.stack([a[:, i * hc : (i + 1) * hc] for a in inputs])
+        hi = jnp.stack([a[:, half + i * hc : half + (i + 1) * hc] for a in inputs])
+        return jnp.where(low, lo, hi)
+
+    received = [
+        lax.ppermute(chunk_of(jnp.logical_not(keep_low), i), "head", partner) for i in range(CHUNKS)
+    ]
     own_parts, back_parts = [], []
+    done = None
     for i in range(CHUNKS):
-        own_i = keep[:, :, i]
-        recv_i = lax.ppermute(send[:, :, i], "head", partner)
+        own_i = chunk_of(keep_low, i)
+        recv_i = received[i]
         first = jnp.where(is_first, own_i, recv_i)
         second = jnp.where(is_first, recv_i, own_i)
         blk = jnp.concatenate([first, second], axis=1)
         kv_prev = lax.ppermute(blk[1:3], ALL_AXES, forward)
+        if done is not None:
+            (blk, kv_prev), _ = lax.optimization_barrier(((blk, kv_prev), done))
         dq, dk_own, dv_own, dk_prev, dv_prev = block_side(
             blk[0], blk[3], kv_prev[0], kv_prev[1], blk[1], blk[2], prev_valid
         )
-        dkv_next = lax.ppermute(
-            jnp.stack([dk_prev, dv_prev]).astype(jnp.bfloat16), ALL_AXES, backward
-        )
+        dkv_prev = jnp.stack([dk_prev, dv_prev]).astype(jnp.bfloat16)
+        done = (dq, dk_own, dv_own, dkv_prev)
+        dkv_next = lax.ppermute(dkv_prev, ALL_AXES, backward)
         dk = dk_own + dkv_next[0].astype(jnp.float32)
         dv = dv_own + dkv_next[1].astype(jnp.float32)
         grads = jnp.stack([dq, dk, dv]).astype(jnp.bfloat16)
@@ -132,12 +140,14 @@
         theirs = jnp.where(is_first, grads[:, rows:], grads[:, :rows])
         own_parts.append(mine)
         back_parts.append(lax.ppermute(theirs, "head", partner))
-    own_all = jnp.stack(own_parts, axis=2)
-    back_all = jnp.stack(back_parts, axis=2)
-    low = jnp.where(keep_low, own_all, back_all)
-    high = jnp.where(keep_low, back_all, own_all)
-    out = jnp.stack([low, high], axis=2).reshape(3, rows, all_heads, hd)
-    return out[0], out[1], out[2]
+    own_all = jnp.concatenate(own_parts, axis=2)
+    back_all = jnp.concatenate(back_parts, axis=2)
+    outs = []
+    for k in range(3):
+        low = jnp.where(keep_low, own_all[k], back_all[k])
+        high = jnp.where(keep_low, back_all[k], own_all[k])
+        outs.append(jnp.concatenate([low, high], axis=1))
+    return tuple(outs)
 
 
 def solution(mesh):

time: 220 us -> 201 us (0.914)
  waiting for transfers between devices: 137 us -> 115 us
  other arithmetic: 11.4 us -> 18.6 us
    ppermute x4, waiting for transfers between devices: 26.9 us -> 9.64 us  [on_device(): kv_prev = lax.ppermute(blk[1:3], ALL_AXES, forward)]
    select_n x2 -> x12, other arithmetic: 1.13 us -> 10.2 us  [the longest x4 4.31 us: chunk_of(): return jnp.where(low, lo, hi)]
    another operation x10 -> x4, other arithmetic: 4.96 us -> 0.3 us  [on_device(): dkv_prev = jnp.stack([dk_prev, dv_prev]).astype(jnp.bfloat16)]
    unnamed x13 -> x68, local copies, waits for them, and re-layouts: 12.6 us -> 8.27 us
    ppermute x4, waiting for transfers between devices: 38.2 us -> 33.9 us  [on_device(): back_parts.append(lax.ppermute(theirs, 'head', partner))]
    slice x0 -> x4, local copies, waits for them, and re-layouts: none -> 3.91 us  [chunk_of(): lo = jnp.stack([a[:, i * hc:(i + 1) * hc] for a in inputs])]
  transfers between devices with their start and end apart: 16 -> 16, of which waited for: 12 -> 10; matrix products, arithmetic and copies ran while one was open for 9% -> 17% of each run, Pallas kernels for 0% -> 0%
where the time goes in v1:
time: 201 us
  waiting for transfers between devices  115 us (57%)
  starting transfers between devices  30.3 us (15%)
  matrix products  21.5 us (11%)
  other arithmetic  18.6 us (9%)
  local copies, waits for them, and re-layouts  13.2 us (7%)
    ppermute x4, waiting for transfers between devices, on_device(): lax.ppermute(chunk_of(jnp.logical_not(keep_low), i), 'head', partner)  53.7 us
    ppermute x4, waiting for transfers between devices, on_device(): back_parts.append(lax.ppermute(theirs, 'head', partner))  33.9 us
    ppermute x4, waiting for transfers between devices, on_device(): dkv_next = lax.ppermute(dkv_prev, ALL_AXES, backward)  18 us
    ppermute x4, starting transfers between devices, on_device(): dkv_next = lax.ppermute(dkv_prev, ALL_AXES, backward)  10.4 us
    ppermute x4, starting transfers between devices, on_device(): kv_prev = lax.ppermute(blk[1:3], ALL_AXES, forward)  10.1 us
    ppermute x4, waiting for transfers between devices, on_device(): kv_prev = lax.ppermute(blk[1:3], ALL_AXES, forward)  9.64 us
    unnamed x68, local copies, waits for them, and re-layouts  8.27 us
    ppermute x4, starting transfers between devices, on_device(): back_parts.append(lax.ppermute(theirs, 'head', partner))  5.56 us
  transfers between devices with their start and end apart: 16, of which 10 were waited for; matrix products, arithmetic and copies ran while one was open for 17% of the time, Pallas kernels for 0%

profile of v1, /device:TPU:24, one launch (start us, length us, event | category | flops | bytes accessed | tf_op | source)
XLA Modules:
  0.0 200.7 jit_solution(16875563749458319730)
XLA Ops:
  0.7 2.5 %fusion.216 = (bf16[128,6,128]{2,1,0:T(8,128)(2,1)S(1)}, bf16[128,6,128]{2,1,0:T(8,128)(2,1)S(1)}, bf16[128,6,128]{2,1,0:T(8,128)(2,1)S(1)}, bf16[128,6,128]{2,1...) fusion(bf16[128,48,128]{2,1,0:T(8,128)(2,1)} %param.7), kind=kLoop, calls=%fused_computation.390 | loop fusion | bytes 3145728 | tf_op jit(solution)/shard_map/slice | solution.py:112
  3.7 0.9 copy-done.1
  5.1 0.9 copy-done.2
  6.7 1.1 broadcast_select_fusion
  7.8 1.5 collective-permute-start.9
  9.7 1.1 broadcast_select_fusion.1
  10.7 0.6 collective-permute-start.6
  11.6 1.1 broadcast_select_fusion.2
  12.7 1.5 collective-permute-start.3
  14.5 0.8 copy-done.27
  15.4 1.1 broadcast_select_fusion.3
  16.5 0.6 collective-permute-start
  17.1 11.4 %collective-permute-done.9 = bf16[4,128,6,128]{3,1,2,0:T(8,128)(2,1)} collective-permute-done((bf16[4,128,6,128]{3,1,2,0:T(8,128)(2,1)}, bf16[4,128,6,128]{3,1,2,0:T(8,128)(2,1)}, u32[]{:S(2)}, u32[]{:S(2)}) %collective-permute-start.9) | collective-permute-done | bytes 786464 | tf_op jit(solution)/shard_map/ppermute | solution.py:117
  28.6 1.4 broadcast_select_fusion.9
  30.1 2.1 %collective-permute-start.10 = (bf16[2,256,6,128]{3,1,2,0:T(8,128)(2,1)S(1)}, bf16[2,256,6,128]{3,1,2,0:T(8,128)(2,1)S(1)}, u32[]{:S(2)}, u32[]{:S(2)}) collective-permute-start(bf16[2,256,6,128]{3,1,2,0:T(8,128)(2,1)S(1)} %fusion.43), channel_id=1, source_target_pairs={{0,1},{1,2},{2,3},{3,4},{4,5},{5,6},{6,7},{7,8},{8,9},{9,10},{10,1... | collective-permute-start | bytes 2359304 | tf_op jit(solution)/shard_map/ppermute | solution.py:127
  32.1 13.3 %collective-permute-done.6 = bf16[4,128,6,128]{3,1,2,0:T(8,128)(2,1)} collective-permute-done((bf16[4,128,6,128]{3,1,2,0:T(8,128)(2,1)}, bf16[4,128,6,128]{3,1,2,0:T(8,128)(2,1)}, u32[]{:S(2)}, u32[]{:S(2)}) %collective-permute-start.6) | collective-permute-done | bytes 786464 | tf_op jit(solution)/shard_map/ppermute | solution.py:117
  45.5 1.4 broadcast_select_fusion.11
  47.0 2.1 %collective-permute-start.7 = (bf16[2,256,6,128]{3,1,2,0:T(8,128)(2,1)S(1)}, bf16[2,256,6,128]{3,1,2,0:T(8,128)(2,1)S(1)}, u32[]{:S(2)}, u32[]{:S(2)}) collective-permute-start(bf16[2,256,6,128]{3,1,2,0:T(8,128)(2,1)S(1)} %fusion.44), channel_id=1, source_target_pairs={{0,1},{1,2},{2,3},{3,4},{4,5},{5,6},{6,7},{7,8},{8,9},{9,10},{10,1... | collective-permute-start | bytes 2359304 | tf_op jit(solution)/shard_map/ppermute | solution.py:127
  49.1 28.9 %collective-permute-done = bf16[4,128,6,128]{3,1,2,0:T(8,128)(2,1)} collective-permute-done((bf16[4,128,6,128]{3,1,2,0:T(8,128)(2,1)}, bf16[4,128,6,128]{3,1,2,0:T(8,128)(2,1)}, u32[]{:S(2)}, u32[]{:S(2)}) %collective-permute-start) | collective-permute-done | bytes 786464 | tf_op jit(solution)/shard_map/ppermute | solution.py:117
  78.1 1.4 broadcast_select_fusion.14
  79.5 1.9 collective-permute-start.1
  81.6 1.4 broadcast_select_fusion.13
  83.0 4.1 %collective-permute-start.4 = (bf16[2,256,6,128]{3,1,2,0:T(8,128)(2,1)S(1)}, bf16[2,256,6,128]{3,1,2,0:T(8,128)(2,1)S(1)}, u32[]{:S(2)}, u32[]{:S(2)}) collective-permute-start(bf16[2,256,6,128]{3,1,2,0:T(8,128)(2,1)S(1)} %fusion.45), channel_id=1, source_target_pairs={{0,1},{1,2},{2,3},{3,4},{4,5},{5,6},{6,7},{7,8},{8,9},{9,10},{10,1... | collective-permute-start | bytes 2359304 | tf_op jit(solution)/shard_map/ppermute | solution.py:127
  88.0 7.0 %collective-permute-done.1 = bf16[2,256,6,128]{3,1,2,0:T(8,128)(2,1)S(1)} collective-permute-done((bf16[2,256,6,128]{3,1,2,0:T(8,128)(2,1)S(1)}, bf16[2,256,6,128]{3,1,2,0:T(8,128)(2,1)S(1)}, u32[]{:S(2)}, u32[]{:S(2)}) %collective-permute-start.1) | collective-permute-done | bytes 786464 | tf_op jit(solution)/shard_map/ppermute | solution.py:127
  95.3 0.6 select_reduce_fusion.12
  96.9 0.7 multiply_reduce_fusion
  100.7 2.7 %collective-permute-done.4 = bf16[2,256,6,128]{3,1,2,0:T(8,128)(2,1)S(1)} collective-permute-done((bf16[2,256,6,128]{3,1,2,0:T(8,128)(2,1)S(1)}, bf16[2,256,6,128]{3,1,2,0:T(8,128)(2,1)S(1)}, u32[]{:S(2)}, u32[]{:S(2)}) %collective-permute-start.4) | collective-permute-done | bytes 786464 | tf_op jit(solution)/shard_map/ppermute | solution.py:127
  105.3 0.7 fusion.31
  110.3 0.8 select_reduce_fusion.4
  111.6 0.7 fusion.32
  118.2 1.9 collective-permute-start.8
  120.2 4.1 %collective-permute-start.5 = (bf16[2,256,6,128]{1,3,2,0:T(8,128)(2,1)S(1)}, bf16[2,256,6,128]{1,3,2,0:T(8,128)(2,1)S(1)}, u32[]{:S(2)}, u32[]{:S(2)}) collective-permute-start(bf16[2,256,6,128]{1,3,2,0:T(8,128)(2,1)S(1)} %pad_maximum_fusion.16), channel_id=1, source_target_pairs={{1,0},{2,1},{3,2},{4,3},{5,4},{6,5},{7,6},{8,7},{9,8},{10,9},{11,1... | collective-permute-start | bytes 2359304 | tf_op jit(solution)/shard_map/ppermute | solution.py:135
  124.3 1.9 collective-permute-start.2
  126.2 0.7 fusion.33
  127.9 2.4 %collective-permute-start.11 = (bf16[2,256,6,128]{1,3,2,0:T(8,128)(2,1)S(1)}, bf16[2,256,6,128]{1,3,2,0:T(8,128)(2,1)S(1)}, u32[]{:S(2)}, u32[]{:S(2)}) collective-permute-start(bf16[2,256,6,128]{1,3,2,0:T(8,128)(2,1)S(1)} %pad_maximum_fusion.22), channel_id=1, source_target_pairs={{1,0},{2,1},{3,2},{4,3},{5,4},{6,5},{7,6},{8,7},{9,8},{10,9},{11,1... | collective-permute-start | bytes 2359304 | tf_op jit(solution)/shard_map/ppermute | solution.py:135
  131.7 6.3 %collective-permute-done.5 = bf16[2,256,6,128]{1,3,2,0:T(8,128)(2,1)S(1)} collective-permute-done((bf16[2,256,6,128]{1,3,2,0:T(8,128)(2,1)S(1)}, bf16[2,256,6,128]{1,3,2,0:T(8,128)(2,1)S(1)}, u32[]{:S(2)}, u32[]{:S(2)}) %collective-permute-start.5) | collective-permute-done | bytes 786464 | tf_op jit(solution)/shard_map/ppermute | solution.py:135
  138.8 1.6 collective-permute-start.14
  140.9 5.6 %collective-permute-done.2 = bf16[2,256,6,128]{1,3,2,0:T(8,128)(2,1)S(1)} collective-permute-done((bf16[2,256,6,128]{1,3,2,0:T(8,128)(2,1)S(1)}, bf16[2,256,6,128]{1,3,2,0:T(8,128)(2,1)S(1)}, u32[]{:S(2)}, u32[]{:S(2)}) %collective-permute-start.2) | collective-permute-done | bytes 786464 | tf_op jit(solution)/shard_map/ppermute | solution.py:135
  147.0 1.9 collective-permute-start.12
  148.8 6.1 %collective-permute-done.11 = bf16[2,256,6,128]{1,3,2,0:T(8,128)(2,1)S(1)} collective-permute-done((bf16[2,256,6,128]{1,3,2,0:T(8,128)(2,1)S(1)}, bf16[2,256,6,128]{1,3,2,0:T(8,128)(2,1)S(1)}, u32[]{:S(2)}, u32[]{:S(2)}) %collective-permute-start.11) | collective-permute-done | bytes 786464 | tf_op jit(solution)/shard_map/ppermute | solution.py:135
  156.0 1.6 collective-permute-start.15
  157.9 22.4 %collective-permute-done.12 = bf16[3,128,6,128]{1,3,2,0:T(8,128)(2,1)S(1)} collective-permute-done((bf16[3,128,6,128]{1,3,2,0:T(8,128)(2,1)S(1)}, bf16[3,128,6,128]{1,3,2,0:T(8,128)(2,1)S(1)}, u32[]{:S(2)}, u32[]{:S(2)}) %collective-permute-start.12) | collective-permute-done | bytes 589856 | tf_op jit(solution)/shard_map/ppermute | solution.py:142
  180.6 11.5 %collective-permute-done.15 = bf16[3,128,6,128]{1,3,2,0:T(8,128)(2,1)S(1)} collective-permute-done((bf16[3,128,6,128]{1,3,2,0:T(8,128)(2,1)S(1)}, bf16[3,128,6,128]{1,3,2,0:T(8,128)(2,1)S(1)}, u32[]{:S(2)}, u32[]{:S(2)}) %collective-permute-start.15) | collective-permute-done | bytes 589856 | tf_op jit(solution)/shard_map/ppermute | solution.py:142
  192.2 1.5 select_bitcast_fusion.1
  193.8 1.7 copy.121
  195.6 1.5 pad_maximum_fusion.5
  197.1 1.7 copy.120
  198.9 1.7 copy.119
  (171 shorter events, 26.5 us)
Async XLA Ops:
  0.6 2.5 %copy-start = (bf16[128,48,128]{2,1,0:T(8,128)(2,1)S(1)}, bf16[128,48,128]{2,1,0:T(8,128)(2,1)}, u32[]{:S(2)}) copy-start(bf16[128,48,128]{2,1,0:T(8,128)(2,1)} %param.6) | copy-start | bytes 4718596
  3.2 1.4 copy-start.1
  4.6 1.4 copy-start.2
  7.8 20.7 %collective-permute-start.9 = (bf16[4,128,6,128]{3,1,2,0:T(8,128)(2,1)}, bf16[4,128,6,128]{3,1,2,0:T(8,128)(2,1)}, u32[]{:S(2)}, u32[]{:S(2)}) collective-permute-start(bf16[4,128,6,128]{3,1,2,0:T(8,128)(2,1)} %broadcast_select_fusion), channel_id=1, source_target_pairs={{0,32},{32,0},{64,96},{96,64},{1,33},{33,1},{65,97},{97,65},{2,34}... | collective-permute-start | bytes 2359304 | tf_op jit(solution)/shard_map/ppermute | solution.py:117
  9.5 1.3 copy-start.3
  9.5 1.3 copy-start.5
  9.5 1.2 copy-start.7
  9.6 1.2 copy-start.9
  9.6 1.8 copy-start.11
  9.6 1.8 copy-start.13
  10.7 34.7 %collective-permute-start.6 = (bf16[4,128,6,128]{3,1,2,0:T(8,128)(2,1)}, bf16[4,128,6,128]{3,1,2,0:T(8,128)(2,1)}, u32[]{:S(2)}, u32[]{:S(2)}) collective-permute-start(bf16[4,128,6,128]{3,1,2,0:T(8,128)(2,1)} %broadcast_select_fusion.1), channel_id=1, source_target_pairs={{0,32},{32,0},{64,96},{96,64},{1,33},{33,1},{65,97},{97,65},{2,34}... | collective-permute-start | bytes 2359304 | tf_op jit(solution)/shard_map/ppermute | solution.py:117
  12.7 68.9 %collective-permute-start.3 = (bf16[4,128,6,128]{3,1,2,0:T(8,128)(2,1)}, bf16[4,128,6,128]{3,1,2,0:T(8,128)(2,1)}, u32[]{:S(2)}, u32[]{:S(2)}) collective-permute-start(bf16[4,128,6,128]{3,1,2,0:T(8,128)(2,1)} %broadcast_select_fusion.2), channel_id=1, source_target_pairs={{0,32},{32,0},{64,96},{96,64},{1,33},{33,1},{65,97},{97,65},{2,34}... | collective-permute-start | bytes 2359304 | tf_op jit(solution)/shard_map/ppermute | solution.py:117
  14.3 2.2 %copy-start.15 = (bf16[1,128,6,128]{3,1,2,0:T(8,128)(2,1)}, bf16[1,128,6,128]{3,1,2,0:T(8,128)(2,1)S(1)}, u32[]{:S(2)}) copy-start(bf16[1,128,6,128]{3,1,2,0:T(8,128)(2,1)S(1)} %get-tuple-element.119) | copy-start | bytes 589828
  14.3 2.2 %copy-start.17 = (bf16[1,128,6,128]{3,1,2,0:T(8,128)(2,1)}, bf16[1,128,6,128]{3,1,2,0:T(8,128)(2,1)S(1)}, u32[]{:S(2)}) copy-start(bf16[1,128,6,128]{3,1,2,0:T(8,128)(2,1)S(1)} %get-tuple-element.120) | copy-start | bytes 589828
  14.3 2.1 %copy-start.19 = (bf16[1,128,6,128]{3,1,2,0:T(8,128)(2,1)}, bf16[1,128,6,128]{3,1,2,0:T(8,128)(2,1)S(1)}, u32[]{:S(2)}) copy-start(bf16[1,128,6,128]{3,1,2,0:T(8,128)(2,1)S(1)} %get-tuple-element.127) | copy-start | bytes 589828
  14.3 2.1 %copy-start.21 = (bf16[1,128,6,128]{3,1,2,0:T(8,128)(2,1)}, bf16[1,128,6,128]{3,1,2,0:T(8,128)(2,1)S(1)}, u32[]{:S(2)}) copy-start(bf16[1,128,6,128]{3,1,2,0:T(8,128)(2,1)S(1)} %get-tuple-element.128) | copy-start | bytes 589828
  14.4 2.0 %copy-start.23 = (bf16[1,128,6,128]{3,1,2,0:T(8,128)(2,1)}, bf16[1,128,6,128]{3,1,2,0:T(8,128)(2,1)S(1)}, u32[]{:S(2)}) copy-start(bf16[1,128,6,128]{3,1,2,0:T(8,128)(2,1)S(1)} %get-tuple-element.135) | copy-start | bytes 589828
  14.4 2.0 %copy-start.25 = (bf16[1,128,6,128]{3,1,2,0:T(8,128)(2,1)}, bf16[1,128,6,128]{3,1,2,0:T(8,128)(2,1)S(1)}, u32[]{:S(2)}) copy-start(bf16[1,128,6,128]{3,1,2,0:T(8,128)(2,1)S(1)} %get-tuple-element.136) | copy-start | bytes 589828
  14.5 0.8 copy-start.27
  14.5 1.9 copy-start.29
  16.5 61.5 %collective-permute-start = (bf16[4,128,6,128]{3,1,2,0:T(8,128)(2,1)}, bf16[4,128,6,128]{3,1,2,0:T(8,128)(2,1)}, u32[]{:S(2)}, u32[]{:S(2)}) collective-permute-start(bf16[4,128,6,128]{3,1,2,0:T(8,128)(2,1)} %broadcast_select_fusion.3), channel_id=1, source_target_pairs={{0,32},{32,0},{64,96},{96,64},{1,33},{33,1},{65,97},{97,65},{2,34}... | collective-permute-start | bytes 2359304 | tf_op jit(solution)/shard_map/ppermute | solution.py:117
  30.0 15.5 %copy-start.4 = (bf16[1,128,6,128]{3,1,2,0:T(8,128)(2,1)S(1)}, bf16[1,128,6,128]{3,1,2,0:T(8,128)(2,1)}, u32[]{:S(2)}) copy-start(bf16[1,128,6,128]{3,1,2,0:T(8,128)(2,1)} %copy-done.3) | copy-start | bytes 589828
  30.0 15.5 %copy-start.6 = (bf16[1,128,6,128]{3,1,2,0:T(8,128)(2,1)S(1)}, bf16[1,128,6,128]{3,1,2,0:T(8,128)(2,1)}, u32[]{:S(2)}) copy-start(bf16[1,128,6,128]{3,1,2,0:T(8,128)(2,1)} %copy-done.5) | copy-start | bytes 589828
  30.0 15.5 %copy-start.8 = (bf16[1,128,6,128]{3,1,2,0:T(8,128)(2,1)S(1)}, bf16[1,128,6,128]{3,1,2,0:T(8,128)(2,1)}, u32[]{:S(2)}) copy-start(bf16[1,128,6,128]{3,1,2,0:T(8,128)(2,1)} %copy-done.7) | copy-start | bytes 589828
  30.0 15.5 %copy-start.10 = (bf16[1,128,6,128]{3,1,2,0:T(8,128)(2,1)S(1)}, bf16[1,128,6,128]{3,1,2,0:T(8,128)(2,1)}, u32[]{:S(2)}) copy-start(bf16[1,128,6,128]{3,1,2,0:T(8,128)(2,1)} %copy-done.9) | copy-start | bytes 589828
  30.0 15.5 %copy-start.12 = (bf16[1,128,6,128]{3,1,2,0:T(8,128)(2,1)S(1)}, bf16[1,128,6,128]{3,1,2,0:T(8,128)(2,1)}, u32[]{:S(2)}) copy-start(bf16[1,128,6,128]{3,1,2,0:T(8,128)(2,1)} %copy-done.11) | copy-start | bytes 589828
  30.0 15.5 %copy-start.14 = (bf16[1,128,6,128]{3,1,2,0:T(8,128)(2,1)S(1)}, bf16[1,128,6,128]{3,1,2,0:T(8,128)(2,1)}, u32[]{:S(2)}) copy-start(bf16[1,128,6,128]{3,1,2,0:T(8,128)(2,1)} %copy-done.13) | copy-start | bytes 589828
  30.1 85.7 %collective-permute-start.10 = (bf16[2,256,6,128]{3,1,2,0:T(8,128)(2,1)S(1)}, bf16[2,256,6,128]{3,1,2,0:T(8,128)(2,1)S(1)}, u32[]{:S(2)}, u32[]{:S(2)}) collective-permute-start(bf16[2,256,6,128]{3,1,2,0:T(8,128)(2,1)S(1)} %fusion.43), channel_id=1, source_target_pairs={{0,1},{1,2},{2,3},{3,4},{4,5},{5,6},{6,7},{7,8},{8,9},{9,10},{10,1... | collective-permute-start | bytes 2359304 | tf_op jit(solution)/shard_map/ppermute | solution.py:127
  46.9 31.1 %copy-start.16 = (bf16[1,128,6,128]{3,1,2,0:T(8,128)(2,1)S(1)}, bf16[1,128,6,128]{3,1,2,0:T(8,128)(2,1)}, u32[]{:S(2)}) copy-start(bf16[1,128,6,128]{3,1,2,0:T(8,128)(2,1)} %copy-done.15) | copy-start | bytes 589828
  46.9 31.1 %copy-start.18 = (bf16[1,128,6,128]{3,1,2,0:T(8,128)(2,1)S(1)}, bf16[1,128,6,128]{3,1,2,0:T(8,128)(2,1)}, u32[]{:S(2)}) copy-start(bf16[1,128,6,128]{3,1,2,0:T(8,128)(2,1)} %copy-done.17) | copy-start | bytes 589828
  46.9 31.1 %copy-start.20 = (bf16[1,128,6,128]{3,1,2,0:T(8,128)(2,1)S(1)}, bf16[1,128,6,128]{3,1,2,0:T(8,128)(2,1)}, u32[]{:S(2)}) copy-start(bf16[1,128,6,128]{3,1,2,0:T(8,128)(2,1)} %copy-done.19) | copy-start | bytes 589828
  46.9 31.1 %copy-start.22 = (bf16[1,128,6,128]{3,1,2,0:T(8,128)(2,1)S(1)}, bf16[1,128,6,128]{3,1,2,0:T(8,128)(2,1)}, u32[]{:S(2)}) copy-start(bf16[1,128,6,128]{3,1,2,0:T(8,128)(2,1)} %copy-done.21) | copy-start | bytes 589828
  46.9 31.1 %copy-start.24 = (bf16[1,128,6,128]{3,1,2,0:T(8,128)(2,1)S(1)}, bf16[1,128,6,128]{3,1,2,0:T(8,128)(2,1)}, u32[]{:S(2)}) copy-start(bf16[1,128,6,128]{3,1,2,0:T(8,128)(2,1)} %copy-done.23) | copy-start | bytes 589828
  46.9 31.1 %copy-start.26 = (bf16[1,128,6,128]{3,1,2,0:T(8,128)(2,1)S(1)}, bf16[1,128,6,128]{3,1,2,0:T(8,128)(2,1)}, u32[]{:S(2)}) copy-start(bf16[1,128,6,128]{3,1,2,0:T(8,128)(2,1)} %copy-done.25) | copy-start | bytes 589828
  46.9 31.1 %copy-start.28 = (bf16[1,128,6,128]{3,1,2,0:T(8,128)(2,1)S(1)}, bf16[1,128,6,128]{3,1,2,0:T(8,128)(2,1)}, u32[]{:S(2)}) copy-start(bf16[1,128,6,128]{3,1,2,0:T(8,128)(2,1)} %copy-done.27) | copy-start | bytes 589828
  46.9 31.1 %copy-start.30 = (bf16[1,128,6,128]{3,1,2,0:T(8,128)(2,1)S(1)}, bf16[1,128,6,128]{3,1,2,0:T(8,128)(2,1)}, u32[]{:S(2)}) copy-start(bf16[1,128,6,128]{3,1,2,0:T(8,128)(2,1)} %copy-done.29) | copy-start | bytes 589828
  47.0 62.5 %collective-permute-start.7 = (bf16[2,256,6,128]{3,1,2,0:T(8,128)(2,1)S(1)}, bf16[2,256,6,128]{3,1,2,0:T(8,128)(2,1)S(1)}, u32[]{:S(2)}, u32[]{:S(2)}) collective-permute-start(bf16[2,256,6,128]{3,1,2,0:T(8,128)(2,1)S(1)} %fusion.44), channel_id=1, source_target_pairs={{0,1},{1,2},{2,3},{3,4},{4,5},{5,6},{6,7},{7,8},{8,9},{9,10},{10,1... | collective-permute-start | bytes 2359304 | tf_op jit(solution)/shard_map/ppermute | solution.py:127
  79.5 15.4 %collective-permute-start.1 = (bf16[2,256,6,128]{3,1,2,0:T(8,128)(2,1)S(1)}, bf16[2,256,6,128]{3,1,2,0:T(8,128)(2,1)S(1)}, u32[]{:S(2)}, u32[]{:S(2)}) collective-permute-start(bf16[2,256,6,128]{3,1,2,0:T(8,128)(2,1)S(1)} %fusion.46), channel_id=1, source_target_pairs={{0,1},{1,2},{2,3},{3,4},{4,5},{5,6},{6,7},{7,8},{8,9},{9,10},{10,1... | collective-permute-start | bytes 2359304 | tf_op jit(solution)/shard_map/ppermute | solution.py:127
  83.0 20.4 %collective-permute-start.4 = (bf16[2,256,6,128]{3,1,2,0:T(8,128)(2,1)S(1)}, bf16[2,256,6,128]{3,1,2,0:T(8,128)(2,1)S(1)}, u32[]{:S(2)}, u32[]{:S(2)}) collective-permute-start(bf16[2,256,6,128]{3,1,2,0:T(8,128)(2,1)S(1)} %fusion.45), channel_id=1, source_target_pairs={{0,1},{1,2},{2,3},{3,4},{4,5},{5,6},{6,7},{7,8},{8,9},{9,10},{10,1... | collective-permute-start | bytes 2359304 | tf_op jit(solution)/shard_map/ppermute | solution.py:127
  118.2 13.2 %collective-permute-start.8 = (bf16[2,256,6,128]{1,3,2,0:T(8,128)(2,1)S(1)}, bf16[2,256,6,128]{1,3,2,0:T(8,128)(2,1)S(1)}, u32[]{:S(2)}, u32[]{:S(2)}) collective-permute-start(bf16[2,256,6,128]{1,3,2,0:T(8,128)(2,1)S(1)} %pad_maximum_fusion.19), channel_id=1, source_target_pairs={{1,0},{2,1},{3,2},{4,3},{5,4},{6,5},{7,6},{8,7},{9,8},{10,9},{11,1... | collective-permute-start | bytes 2359304 | tf_op jit(solution)/shard_map/ppermute | solution.py:135
  120.2 17.9 %collective-permute-start.5 = (bf16[2,256,6,128]{1,3,2,0:T(8,128)(2,1)S(1)}, bf16[2,256,6,128]{1,3,2,0:T(8,128)(2,1)S(1)}, u32[]{:S(2)}, u32[]{:S(2)}) collective-permute-start(bf16[2,256,6,128]{1,3,2,0:T(8,128)(2,1)S(1)} %pad_maximum_fusion.16), channel_id=1, source_target_pairs={{1,0},{2,1},{3,2},{4,3},{5,4},{6,5},{7,6},{8,7},{9,8},{10,9},{11,1... | collective-permute-start | bytes 2359304 | tf_op jit(solution)/shard_map/ppermute | solution.py:135
  124.3 22.2 %collective-permute-start.2 = (bf16[2,256,6,128]{1,3,2,0:T(8,128)(2,1)S(1)}, bf16[2,256,6,128]{1,3,2,0:T(8,128)(2,1)S(1)}, u32[]{:S(2)}, u32[]{:S(2)}) collective-permute-start(bf16[2,256,6,128]{1,3,2,0:T(8,128)(2,1)S(1)} %pad_maximum_fusion.13), channel_id=1, source_target_pairs={{1,0},{2,1},{3,2},{4,3},{5,4},{6,5},{7,6},{8,7},{9,8},{10,9},{11,1... | collective-permute-start | bytes 2359304 | tf_op jit(solution)/shard_map/ppermute | solution.py:135
  127.9 27.0 %collective-permute-start.11 = (bf16[2,256,6,128]{1,3,2,0:T(8,128)(2,1)S(1)}, bf16[2,256,6,128]{1,3,2,0:T(8,128)(2,1)S(1)}, u32[]{:S(2)}, u32[]{:S(2)}) collective-permute-start(bf16[2,256,6,128]{1,3,2,0:T(8,128)(2,1)S(1)} %pad_maximum_fusion.22), channel_id=1, source_target_pairs={{1,0},{2,1},{3,2},{4,3},{5,4},{6,5},{7,6},{8,7},{9,8},{10,9},{11,1... | collective-permute-start | bytes 2359304 | tf_op jit(solution)/shard_map/ppermute | solution.py:135
  138.8 41.7 %collective-permute-start.14 = (bf16[3,128,6,128]{1,3,2,0:T(8,128)(2,1)S(1)}, bf16[3,128,6,128]{1,3,2,0:T(8,128)(2,1)S(1)}, u32[]{:S(2)}, u32[]{:S(2)}) collective-permute-start(bf16[3,128,6,128]{1,3,2,0:T(8,128)(2,1)S(1)} %get-tuple-element.80), channel_id=1, source_target_pairs={{0,32},{32,0},{64,96},{96,64},{1,33},{33,1},{65,97},{97,65},{2,34}... | collective-permute-start | bytes 1769480 | tf_op jit(solution)/shard_map/ppermute | solution.py:142
  140.4 40.0 %collective-permute-start.13 = (bf16[3,128,6,128]{1,3,2,0:T(8,128)(2,1)S(1)}, bf16[3,128,6,128]{1,3,2,0:T(8,128)(2,1)S(1)}, u32[]{:S(2)}, u32[]{:S(2)}) collective-permute-start(bf16[3,128,6,128]{1,3,2,0:T(8,128)(2,1)S(1)} %get-tuple-element.78), channel_id=1, source_target_pairs={{0,32},{32,0},{64,96},{96,64},{1,33},{33,1},{65,97},{97,65},{2,34}... | collective-permute-start | bytes 1769480 | tf_op jit(solution)/shard_map/ppermute | solution.py:142
  147.0 33.3 %collective-permute-start.12 = (bf16[3,128,6,128]{1,3,2,0:T(8,128)(2,1)S(1)}, bf16[3,128,6,128]{1,3,2,0:T(8,128)(2,1)S(1)}, u32[]{:S(2)}, u32[]{:S(2)}) collective-permute-start(bf16[3,128,6,128]{1,3,2,0:T(8,128)(2,1)S(1)} %get-tuple-element.76), channel_id=1, source_target_pairs={{0,32},{32,0},{64,96},{96,64},{1,33},{33,1},{65,97},{97,65},{2,34}... | collective-permute-start | bytes 1769480 | tf_op jit(solution)/shard_map/ppermute | solution.py:142
  156.0 36.1 %collective-permute-start.15 = (bf16[3,128,6,128]{1,3,2,0:T(8,128)(2,1)S(1)}, bf16[3,128,6,128]{1,3,2,0:T(8,128)(2,1)S(1)}, u32[]{:S(2)}, u32[]{:S(2)}) collective-permute-start(bf16[3,128,6,128]{1,3,2,0:T(8,128)(2,1)S(1)} %get-tuple-element.82), channel_id=1, source_target_pairs={{0,32},{32,0},{64,96},{96,64},{1,33},{33,1},{65,97},{97,65},{2,34}... | collective-permute-start | bytes 1769480 | tf_op jit(solution)/shard_map/ppermute | solution.py:142

commit v2 on v1

--- a/solution.py
+++ b/solution.py
@@ -4,6 +4,7 @@
 from jax.sharding import PartitionSpec as P
 
 CHUNKS = 4
+GROUP = 2
 ALL_AXES = ("head", "ctx", "inner")
 
 
@@ -99,6 +100,7 @@
     keep_low = (h == 1) | (h == 2)
     is_first = h % 2 == 0
     prev_valid = (h >= heads // 2) | (c > 0)
+    sender_first = is_first ^ ((h >= heads // 2) & (c == cycle - 1))
     partner = [(i, i ^ 1) for i in range(heads)]
     forward = halo_pairs(heads, cycle)
     backward = [(t, s) for s, t in forward]
@@ -108,31 +110,53 @@
     hc = half // CHUNKS
     inputs = (query_rows, key_rows, value_rows, grad_rows)
 
-    def chunk_of(low, i):
-        lo = jnp.stack([a[:, i * hc : (i + 1) * hc] for a in inputs])
-        hi = jnp.stack([a[:, half + i * hc : half + (i + 1) * hc] for a in inputs])
+    def chunk_of(arrays, low, i):
+        lo = jnp.stack([a[:, i * hc : (i + 1) * hc] for a in arrays])
+        hi = jnp.stack([a[:, half + i * hc : half + (i + 1) * hc] for a in arrays])
         return jnp.where(low, lo, hi)
 
-    received = [
-        lax.ppermute(chunk_of(jnp.logical_not(keep_low), i), "head", partner) for i in range(CHUNKS)
+    kv_kept = jnp.stack(
+        [chunk_of((key_rows, value_rows), keep_low, i) for i in range(CHUNKS)]
+    )
+    kv_own_prev = lax.ppermute(kv_kept, ALL_AXES, forward)
+    groups = [
+        lax.ppermute(
+            jnp.concatenate(
+                [chunk_of(inputs, jnp.logical_not(keep_low), i) for i in range(g, g + GROUP)], axis=2
+            ),
+            "head",
+            partner,
+        )
+        for g in range(0, CHUNKS, GROUP)
     ]
-    own_parts, back_parts = [], []
-    done = None
+    own_parts, back_parts, returned = [], [], []
+    forwarded = None
     for i in range(CHUNKS):
-        own_i = chunk_of(keep_low, i)
-        recv_i = received[i]
+        own_i = chunk_of(inputs, keep_low, i)
+        if i % GROUP == 0:
+            recv_g = groups[i // GROUP]
+            if i:
+                recv_g, _ = lax.optimization_barrier((recv_g, own_parts[-1]))
+            forwarded = lax.ppermute(recv_g[1:3], ALL_AXES, forward)
+        j = i % GROUP
+        recv_i = recv_g[:, :, j * hc : (j + 1) * hc]
+        kv_other_prev = forwarded[:, :, j * hc : (j + 1) * hc]
         first = jnp.where(is_first, own_i, recv_i)
         second = jnp.where(is_first, recv_i, own_i)
         blk = jnp.concatenate([first, second], axis=1)
-        kv_prev = lax.ppermute(blk[1:3], ALL_AXES, forward)
-        if done is not None:
-            (blk, kv_prev), _ = lax.optimization_barrier(((blk, kv_prev), done))
+        kv_a = jnp.where(sender_first, kv_own_prev[i], kv_other_prev)
+        kv_b = jnp.where(sender_first, kv_other_prev, kv_own_prev[i])
+        kv_prev = jnp.concatenate([kv_a, kv_b], axis=1)
+        waits = tuple(returned[-1:]) + tuple(back_parts[-2:-1])
+        if waits:
+            (blk, kv_prev), _ = lax.optimization_barrier(((blk, kv_prev), waits))
         dq, dk_own, dv_own, dk_prev, dv_prev = block_side(
             blk[0], blk[3], kv_prev[0], kv_prev[1], blk[1], blk[2], prev_valid
         )
-        dkv_prev = jnp.stack([dk_prev, dv_prev]).astype(jnp.bfloat16)
-        done = (dq, dk_own, dv_own, dkv_prev)
-        dkv_next = lax.ppermute(dkv_prev, ALL_AXES, backward)
+        dkv_next = lax.ppermute(
+            jnp.stack([dk_prev, dv_prev]).astype(jnp.bfloat16), ALL_AXES, backward
+        )
+        returned.append(dkv_next)
         dk = dk_own + dkv_next[0].astype(jnp.float32)
         dv = dv_own + dkv_next[1].astype(jnp.float32)
         grads = jnp.stack([dq, dk, dv]).astype(jnp.bfloat16)

time: 201 us -> 181 us (0.900)
  waiting for transfers between devices: 115 us -> 90.8 us
  local copies, waits for them, and re-layouts: 13.2 us -> 17.8 us
    ppermute x4, waiting for transfers between devices: 33.9 us -> 13.1 us  [on_device(): back_parts.append(lax.ppermute(theirs, 'head', partner))]
    unnamed x68 -> x164, local copies, waits for them, and re-layouts: 8.27 us -> 13.9 us
    ppermute x12 -> x9, waiting for transfers between devices: 81.3 us -> 77.7 us  [the longest x2 28.8 us: on_device(): lax.ppermute(jnp.concatenate([chunk_of(inputs, jnp.logical_not(keep_low),...]
    select_n x4, other arithmetic: 4.31 us -> 1.09 us  [chunk_of(): return jnp.where(low, lo, hi)]
    select_n x3 -> x4, other arithmetic: 4.1 us -> 1.01 us  [on_device(): first = jnp.where(is_first, own_i, recv_i)]
    concatenate x0 -> x5, other arithmetic: none -> 2.72 us  [the longest x2 2.56 us: on_device(): jnp.concatenate([chunk_of(inputs, jnp.logical_not(keep_low), i) for i in...]
    select_n x0 -> x2, other arithmetic: none -> 2.44 us  [on_device(): kv_a = jnp.where(sender_first, kv_own_prev[i], kv_other_prev)]
    ppermute x12 -> x9, starting transfers between devices: 24.7 us -> 23.8 us  [the longest x4 15.9 us: on_device(): lax.ppermute(jnp.stack([dk_prev, dv_prev]).astype(jnp.bfloat16), ALL_AXES...]
  transfers between devices with their start and end apart: 16 -> 13, of which waited for: 10 -> 9; matrix products, arithmetic and copies ran while one was open for 17% -> 17% of each run, Pallas kernels for 0% -> 0%
where the time goes in v2:
time: 181 us; the launch traced here: 180 us
  waiting for transfers between devices  90.8 us (50%)
  starting transfers between devices  30.5 us (17%)
  matrix products  21.5 us (12%)
  local copies, waits for them, and re-layouts  17.8 us (10%)
  other arithmetic  17.2 us (10%)
  between operations  2.39 us (1%)
    ppermute x2, waiting for transfers between devices, on_device(): lax.ppermute(jnp.concatenate([chunk_of(inputs, jnp.logical_not(keep_low),...  28.8 us
    ppermute x4, waiting for transfers between devices, on_device(): lax.ppermute(jnp.stack([dk_prev, dv_prev]).astype(jnp.bfloat16), ALL_AXES...  27.3 us
    ppermute x2, waiting for transfers between devices, on_device(): forwarded = lax.ppermute(recv_g[1:3], ALL_AXES, forward)  21.5 us
    ppermute x4, starting transfers between devices, on_device(): lax.ppermute(jnp.stack([dk_prev, dv_prev]).astype(jnp.bfloat16), ALL_AXES...  15.9 us
    unnamed x164, local copies, waits for them, and re-layouts  13.9 us
    ppermute x4, waiting for transfers between devices, on_device(): back_parts.append(lax.ppermute(theirs, 'head', partner))  13.1 us
    ppermute x4, starting transfers between devices, on_device(): back_parts.append(lax.ppermute(theirs, 'head', partner))  6.75 us
    ppermute x2, starting transfers between devices, on_device(): forwarded = lax.ppermute(recv_g[1:3], ALL_AXES, forward)  3.97 us
  transfers between devices with their start and end apart: 13, of which 9 were waited for; matrix products, arithmetic and copies ran while one was open for 17% of the time, Pallas kernels for 0%

profile of v2, /device:TPU:24, one launch (start us, length us, event | category | flops | bytes accessed | tf_op | source)
XLA Modules:
  0.0 180.3 jit_solution(13409304885823098288)
XLA Ops:
  0.6 2.4 %fusion.233 = (bf16[128,6,128]{2,1,0:T(8,128)(2,1)S(1)}, bf16[128,6,128]{2,1,0:T(8,128)(2,1)S(1)}, bf16[128,6,128]{2,1,0:T(8,128)(2,1)S(1)}, bf16[128,6,128]{2,1...) fusion(bf16[128,48,128]{2,1,0:T(8,128)(2,1)} %param.4), kind=kLoop, calls=%fused_computation.420 | loop fusion | bytes 3145728 | tf_op jit(solution)/shard_map/slice | solution.py:114
  3.2 1.4 copy-done.60
  5.3 1.4 copy-done.61
  7.4 1.4 copy-done.62
  10.2 1.3 pad_maximum_fusion.2
  11.5 1.5 collective-permute-start.1
  13.7 1.3 pad_maximum_fusion.1
  15.0 1.9 %collective-permute-start = (bf16[4,2,128,6,128]{4,2,3,1,0:T(8,128)(2,1)}, bf16[4,2,128,6,128]{4,2,3,1,0:T(8,128)(2,1)}, u32[]{:S(2)}, u32[]{:S(2)}) collective-permute-start(bf16[4,2,128,6,128]{4,2,3,1,0:T(8,128)(2,1)} %pad_maximum_fusion.1), channel_id=1, source_target_pairs={{0,1},{1,2},{2,3},{3,4},{4,5},{5,6},{6,7},{7,8},{8,9},{9,10},{10,1... | collective-permute-start | bytes 4718600 | tf_op jit(solution)/shard_map/ppermute | solution.py:121
  18.2 1.3 pad_maximum_fusion.4
  19.5 0.5 collective-permute-start.5
  20.1 28.8 %collective-permute-done.1 = bf16[4,128,12,128]{3,1,2,0:T(8,128)(2,1)S(1)} collective-permute-done((bf16[4,128,12,128]{3,1,2,0:T(8,128)(2,1)}, bf16[4,128,12,128]{3,1,2,0:T(8,128)(2,1)S(1)}, u32[]{:S(2)}, u32[]{:S(2)}) %collective-permute-start.1) | collective-permute-done | bytes 1572896 | tf_op jit(solution)/shard_map/ppermute | solution.py:123
  49.0 1.9 %collective-permute-start.2 = (bf16[2,128,12,128]{3,1,2,0:T(8,128)(2,1)S(1)}, bf16[2,128,12,128]{3,1,2,0:T(8,128)(2,1)S(1)}, u32[]{:S(2)}, u32[]{:S(2)}) collective-permute-start(bf16[2,128,12,128]{3,1,2,0:T(8,128)(2,1)S(1)} %slice.435), channel_id=1, source_target_pairs={{0,1},{1,2},{2,3},{3,4},{4,5},{5,6},{6,7},{7,8},{8,9},{9,10},{10,1... | collective-permute-start | bytes 2359304 | tf_op jit(solution)/shard_map/ppermute | solution.py:140
  51.6 0.6 copy-done.13
  53.9 10.5 %collective-permute-done.2 = bf16[2,128,12,128]{3,1,2,0:T(8,128)(2,1)S(1)} collective-permute-done((bf16[2,128,12,128]{3,1,2,0:T(8,128)(2,1)S(1)}, bf16[2,128,12,128]{3,1,2,0:T(8,128)(2,1)S(1)}, u32[]{:S(2)}, u32[]{:S(2)}) %collective-permute-start.2) | collective-permute-done | bytes 786464 | tf_op jit(solution)/shard_map/ppermute | solution.py:140
  64.4 1.2 broadcast_select_fusion.29
  66.1 0.6 select_reduce_fusion.12
  67.7 0.7 fusion.32
  69.4 2.1 %collective-permute-start.3 = (bf16[2,256,6,128]{1,3,2,0:T(8,128)(2,1)S(1)}, bf16[2,256,6,128]{1,3,2,0:T(8,128)(2,1)S(1)}, u32[]{:S(2)}, u32[]{:S(2)}) collective-permute-start(bf16[2,256,6,128]{1,3,2,0:T(8,128)(2,1)S(1)} %pad_maximum_fusion.18), channel_id=1, source_target_pairs={{1,0},{2,1},{3,2},{4,3},{5,4},{6,5},{7,6},{8,7},{9,8},{10,9},{11,1... | collective-permute-start | bytes 2359304 | tf_op jit(solution)/shard_map/ppermute | solution.py:156
  72.7 8.1 %collective-permute-done.3 = bf16[2,256,6,128]{1,3,2,0:T(8,128)(2,1)S(1)} collective-permute-done((bf16[2,256,6,128]{1,3,2,0:T(8,128)(2,1)S(1)}, bf16[2,256,6,128]{1,3,2,0:T(8,128)(2,1)S(1)}, u32[]{:S(2)}, u32[]{:S(2)}) %collective-permute-start.3) | collective-permute-done | bytes 786464 | tf_op jit(solution)/shard_map/ppermute | solution.py:156
  81.6 0.6 select_reduce_fusion.8
  82.6 0.5 fusion.120
  83.2 0.7 fusion.33
  84.8 5.9 %collective-permute-start.4 = (bf16[2,256,6,128]{1,3,2,0:T(8,128)(2,1)S(1)}, bf16[2,256,6,128]{1,3,2,0:T(8,128)(2,1)S(1)}, u32[]{:S(2)}, u32[]{:S(2)}) collective-permute-start(bf16[2,256,6,128]{1,3,2,0:T(8,128)(2,1)S(1)} %pad_maximum_fusion.20), channel_id=1, source_target_pairs={{1,0},{2,1},{3,2},{4,3},{5,4},{6,5},{7,6},{8,7},{9,8},{10,9},{11,1... | collective-permute-start | bytes 2359304 | tf_op jit(solution)/shard_map/ppermute | solution.py:156
  91.9 1.6 collective-permute-start.7
  94.6 5.6 %collective-permute-done.4 = bf16[2,256,6,128]{1,3,2,0:T(8,128)(2,1)S(1)} collective-permute-done((bf16[2,256,6,128]{1,3,2,0:T(8,128)(2,1)S(1)}, bf16[2,256,6,128]{1,3,2,0:T(8,128)(2,1)S(1)}, u32[]{:S(2)}, u32[]{:S(2)}) %collective-permute-start.4) | collective-permute-done | bytes 786464 | tf_op jit(solution)/shard_map/ppermute | solution.py:156
  101.5 0.7 copy-done.5
  103.4 2.1 %collective-permute-start.6 = (bf16[2,128,12,128]{3,1,2,0:T(8,128)(2,1)S(1)}, bf16[2,128,12,128]{3,1,2,0:T(8,128)(2,1)S(1)}, u32[]{:S(2)}, u32[]{:S(2)}) collective-permute-start(bf16[2,128,12,128]{3,1,2,0:T(8,128)(2,1)S(1)} %slice.403), channel_id=1, source_target_pairs={{0,1},{1,2},{2,3},{3,4},{4,5},{5,6},{6,7},{7,8},{8,9},{9,10},{10,1... | collective-permute-start | bytes 2359304 | tf_op jit(solution)/shard_map/ppermute | solution.py:140
  105.8 1.8 collective-permute-start.9
  108.1 11.0 %collective-permute-done.6 = bf16[2,128,12,128]{3,1,2,0:T(8,128)(2,1)S(1)} collective-permute-done((bf16[2,128,12,128]{3,1,2,0:T(8,128)(2,1)S(1)}, bf16[2,128,12,128]{3,1,2,0:T(8,128)(2,1)S(1)}, u32[]{:S(2)}, u32[]{:S(2)}) %collective-permute-start.6) | collective-permute-done | bytes 786464 | tf_op jit(solution)/shard_map/ppermute | solution.py:140
  119.1 1.2 broadcast_select_fusion.25
  121.2 0.6 select_reduce_fusion.4
  122.8 0.7 fusion.34
  124.5 1.9 %collective-permute-start.8 = (bf16[2,256,6,128]{1,3,2,0:T(8,128)(2,1)S(1)}, bf16[2,256,6,128]{1,3,2,0:T(8,128)(2,1)S(1)}, u32[]{:S(2)}, u32[]{:S(2)}) collective-permute-start(bf16[2,256,6,128]{1,3,2,0:T(8,128)(2,1)S(1)} %pad_maximum_fusion.26), channel_id=1, source_target_pairs={{1,0},{2,1},{3,2},{4,3},{5,4},{6,5},{7,6},{8,7},{9,8},{10,9},{11,1... | collective-permute-start | bytes 2359304 | tf_op jit(solution)/shard_map/ppermute | solution.py:156
  127.7 8.3 %collective-permute-done.8 = bf16[2,256,6,128]{1,3,2,0:T(8,128)(2,1)S(1)} collective-permute-done((bf16[2,256,6,128]{1,3,2,0:T(8,128)(2,1)S(1)}, bf16[2,256,6,128]{1,3,2,0:T(8,128)(2,1)S(1)}, u32[]{:S(2)}, u32[]{:S(2)}) %collective-permute-start.8) | collective-permute-done | bytes 786464 | tf_op jit(solution)/shard_map/ppermute | solution.py:156
  136.7 0.6 select_reduce_fusion
  137.8 0.5 fusion.76
  138.3 0.7 fusion.35
  140.0 5.9 %collective-permute-start.10 = (bf16[2,256,6,128]{1,3,2,0:T(8,128)(2,1)S(1)}, bf16[2,256,6,128]{1,3,2,0:T(8,128)(2,1)S(1)}, u32[]{:S(2)}, u32[]{:S(2)}) collective-permute-start(bf16[2,256,6,128]{1,3,2,0:T(8,128)(2,1)S(1)} %pad_maximum_fusion.28), channel_id=1, source_target_pairs={{1,0},{2,1},{3,2},{4,3},{5,4},{6,5},{7,6},{8,7},{9,8},{10,9},{11,1... | collective-permute-start | bytes 2359304 | tf_op jit(solution)/shard_map/ppermute | solution.py:156
  147.1 1.8 %collective-permute-start.11 = (bf16[3,128,6,128]{1,3,2,0:T(8,128)(2,1)S(1)}, bf16[3,128,6,128]{1,3,2,0:T(8,128)(2,1)S(1)}, u32[]{:S(2)}, u32[]{:S(2)}) collective-permute-start(bf16[3,128,6,128]{1,3,2,0:T(8,128)(2,1)S(1)} %get-tuple-element.80), channel_id=1, source_target_pairs={{0,32},{32,0},{64,96},{96,64},{1,33},{33,1},{65,97},{97,65},{2,34}... | collective-permute-start | bytes 1769480 | tf_op jit(solution)/shard_map/ppermute | solution.py:166
  150.1 5.4 %collective-permute-done.10 = bf16[2,256,6,128]{1,3,2,0:T(8,128)(2,1)S(1)} collective-permute-done((bf16[2,256,6,128]{1,3,2,0:T(8,128)(2,1)S(1)}, bf16[2,256,6,128]{1,3,2,0:T(8,128)(2,1)S(1)}, u32[]{:S(2)}, u32[]{:S(2)}) %collective-permute-start.10) | collective-permute-done | bytes 786464 | tf_op jit(solution)/shard_map/ppermute | solution.py:156
  156.6 1.6 collective-permute-start.12
  158.3 5.4 %collective-permute-done.11 = bf16[3,128,6,128]{1,3,2,0:T(8,128)(2,1)S(1)} collective-permute-done((bf16[3,128,6,128]{1,3,2,0:T(8,128)(2,1)S(1)}, bf16[3,128,6,128]{1,3,2,0:T(8,128)(2,1)S(1)}, u32[]{:S(2)}, u32[]{:S(2)}) %collective-permute-start.11) | collective-permute-done | bytes 589856 | tf_op jit(solution)/shard_map/ppermute | solution.py:166
  164.1 7.7 %collective-permute-done.12 = bf16[3,128,6,128]{1,3,2,0:T(8,128)(2,1)S(1)} collective-permute-done((bf16[3,128,6,128]{1,3,2,0:T(8,128)(2,1)S(1)}, bf16[3,128,6,128]{1,3,2,0:T(8,128)(2,1)S(1)}, u32[]{:S(2)}, u32[]{:S(2)}) %collective-permute-start.12) | collective-permute-done | bytes 589856 | tf_op jit(solution)/shard_map/ppermute | solution.py:166
  171.9 1.4 select_bitcast_fusion.1
  173.5 1.7 copy.121
  175.2 1.5 pad_maximum_fusion.7
  176.7 1.7 copy.119
  178.6 1.7 copy.120
  (252 shorter events, 28.0 us)
Async XLA Ops:
  3.0 1.6 copy-start.60
  3.1 6.4 %copy-start.44 = (bf16[128,6,128]{2,0,1:T(8,128)(2,1)}, bf16[128,6,128]{2,0,1:T(8,128)(2,1)S(1)}, u32[]{:S(2)}) copy-start(bf16[128,6,128]{2,0,1:T(8,128)(2,1)S(1)} %copy.291) | copy-start | bytes 589828
  3.1 6.4 %copy-start.46 = (bf16[128,6,128]{2,0,1:T(8,128)(2,1)}, bf16[128,6,128]{2,0,1:T(8,128)(2,1)S(1)}, u32[]{:S(2)}) copy-start(bf16[128,6,128]{2,0,1:T(8,128)(2,1)S(1)} %copy.293) | copy-start | bytes 589828
  3.2 6.3 %copy-start.48 = (bf16[128,6,128]{2,0,1:T(8,128)(2,1)}, bf16[128,6,128]{2,0,1:T(8,128)(2,1)S(1)}, u32[]{:S(2)}) copy-start(bf16[128,6,128]{2,0,1:T(8,128)(2,1)S(1)} %copy.295) | copy-start | bytes 589828
  4.6 4.9 %copy-start.50 = (bf16[128,6,128]{2,0,1:T(8,128)(2,1)}, bf16[128,6,128]{2,0,1:T(8,128)(2,1)S(1)}, u32[]{:S(2)}) copy-start(bf16[128,6,128]{2,0,1:T(8,128)(2,1)S(1)} %copy.297) | copy-start | bytes 589828
  5.1 1.6 copy-start.61
  5.2 8.3 %copy-start.12 = (bf16[128,6,128]{2,0,1:T(8,128)(2,1)}, bf16[128,6,128]{2,0,1:T(8,128)(2,1)S(1)}, u32[]{:S(2)}) copy-start(bf16[128,6,128]{2,0,1:T(8,128)(2,1)S(1)} %copy.307) | copy-start | bytes 589828
  5.2 8.3 %copy-start.14 = (bf16[128,6,128]{2,0,1:T(8,128)(2,1)}, bf16[128,6,128]{2,0,1:T(8,128)(2,1)S(1)}, u32[]{:S(2)}) copy-start(bf16[128,6,128]{2,0,1:T(8,128)(2,1)S(1)} %copy.309) | copy-start | bytes 589828
  5.2 8.2 %copy-start.20 = (bf16[128,6,128]{2,0,1:T(8,128)(2,1)}, bf16[128,6,128]{2,0,1:T(8,128)(2,1)S(1)}, u32[]{:S(2)}) copy-start(bf16[128,6,128]{2,0,1:T(8,128)(2,1)S(1)} %copy.311) | copy-start | bytes 589828
  6.7 6.8 %copy-start.22 = (bf16[128,6,128]{2,0,1:T(8,128)(2,1)}, bf16[128,6,128]{2,0,1:T(8,128)(2,1)S(1)}, u32[]{:S(2)}) copy-start(bf16[128,6,128]{2,0,1:T(8,128)(2,1)S(1)} %copy.313) | copy-start | bytes 589828
  7.2 1.6 copy-start.62
  7.2 6.3 %copy-start.16 = (bf16[128,6,128]{2,0,1:T(8,128)(2,1)}, bf16[128,6,128]{2,0,1:T(8,128)(2,1)S(1)}, u32[]{:S(2)}) copy-start(bf16[128,6,128]{2,0,1:T(8,128)(2,1)S(1)} %copy.306) | copy-start | bytes 589828
  7.3 6.2 %copy-start.18 = (bf16[128,6,128]{2,0,1:T(8,128)(2,1)}, bf16[128,6,128]{2,0,1:T(8,128)(2,1)S(1)}, u32[]{:S(2)}) copy-start(bf16[128,6,128]{2,0,1:T(8,128)(2,1)S(1)} %copy.308) | copy-start | bytes 589828
  7.3 6.2 %copy-start.24 = (bf16[128,6,128]{2,0,1:T(8,128)(2,1)}, bf16[128,6,128]{2,0,1:T(8,128)(2,1)S(1)}, u32[]{:S(2)}) copy-start(bf16[128,6,128]{2,0,1:T(8,128)(2,1)S(1)} %copy.310) | copy-start | bytes 589828
  8.8 4.7 %copy-start.26 = (bf16[128,6,128]{2,0,1:T(8,128)(2,1)}, bf16[128,6,128]{2,0,1:T(8,128)(2,1)S(1)}, u32[]{:S(2)}) copy-start(bf16[128,6,128]{2,0,1:T(8,128)(2,1)S(1)} %copy.312) | copy-start | bytes 589828
  11.5 37.5 %collective-permute-start.1 = (bf16[4,128,12,128]{3,1,2,0:T(8,128)(2,1)}, bf16[4,128,12,128]{3,1,2,0:T(8,128)(2,1)S(1)}, u32[]{:S(2)}, u32[]{:S(2)}) collective-permute-start(bf16[4,128,12,128]{3,1,2,0:T(8,128)(2,1)} %pad_maximum_fusion.2), channel_id=1, source_target_pairs={{0,32},{32,0},{64,96},{96,64},{1,33},{33,1},{65,97},{97,65},{2,34}... | collective-permute-start | bytes 4718600 | tf_op jit(solution)/shard_map/ppermute | solution.py:123
  13.0 4.3 %copy-start.4 = (bf16[128,6,128]{2,0,1:T(8,128)(2,1)}, bf16[128,6,128]{2,0,1:T(8,128)(2,1)S(1)}, u32[]{:S(2)}) copy-start(bf16[128,6,128]{2,0,1:T(8,128)(2,1)S(1)} %copy.303) | copy-start | bytes 589828
  13.1 4.2 %copy-start.6 = (bf16[128,6,128]{2,0,1:T(8,128)(2,1)}, bf16[128,6,128]{2,0,1:T(8,128)(2,1)S(1)}, u32[]{:S(2)}) copy-start(bf16[128,6,128]{2,0,1:T(8,128)(2,1)S(1)} %copy.305) | copy-start | bytes 589828
  13.2 4.2 %copy-start.8 = (bf16[128,6,128]{2,0,1:T(8,128)(2,1)}, bf16[128,6,128]{2,0,1:T(8,128)(2,1)S(1)}, u32[]{:S(2)}) copy-start(bf16[128,6,128]{2,0,1:T(8,128)(2,1)S(1)} %copy.302) | copy-start | bytes 589828
  13.2 4.1 %copy-start = (bf16[128,6,128]{2,0,1:T(8,128)(2,1)}, bf16[128,6,128]{2,0,1:T(8,128)(2,1)S(1)}, u32[]{:S(2)}) copy-start(bf16[128,6,128]{2,0,1:T(8,128)(2,1)S(1)} %copy.300) | copy-start | bytes 589828
  13.3 4.1 %copy-start.10 = (bf16[128,6,128]{2,0,1:T(8,128)(2,1)}, bf16[128,6,128]{2,0,1:T(8,128)(2,1)S(1)}, u32[]{:S(2)}) copy-start(bf16[128,6,128]{2,0,1:T(8,128)(2,1)S(1)} %copy.304) | copy-start | bytes 589828
  13.3 4.0 %copy-start.2 = (bf16[128,6,128]{2,0,1:T(8,128)(2,1)}, bf16[128,6,128]{2,0,1:T(8,128)(2,1)S(1)}, u32[]{:S(2)}) copy-start(bf16[128,6,128]{2,0,1:T(8,128)(2,1)S(1)} %copy.298) | copy-start | bytes 589828
  15.0 38.9 %collective-permute-start = (bf16[4,2,128,6,128]{4,2,3,1,0:T(8,128)(2,1)}, bf16[4,2,128,6,128]{4,2,3,1,0:T(8,128)(2,1)}, u32[]{:S(2)}, u32[]{:S(2)}) collective-permute-start(bf16[4,2,128,6,128]{4,2,3,1,0:T(8,128)(2,1)} %pad_maximum_fusion.1), channel_id=1, source_target_pairs={{0,1},{1,2},{2,3},{3,4},{4,5},{5,6},{6,7},{7,8},{8,9},{9,10},{10,1... | collective-permute-start | bytes 4718600 | tf_op jit(solution)/shard_map/ppermute | solution.py:121
  19.5 82.0 %collective-permute-start.5 = (bf16[4,128,12,128]{3,1,2,0:T(8,128)(2,1)}, bf16[4,128,12,128]{3,1,2,0:T(8,128)(2,1)S(1)}, u32[]{:S(2)}, u32[]{:S(2)}) collective-permute-start(bf16[4,128,12,128]{3,1,2,0:T(8,128)(2,1)} %pad_maximum_fusion.4), channel_id=1, source_target_pairs={{0,32},{32,0},{64,96},{96,64},{1,33},{33,1},{65,97},{97,65},{2,34}... | collective-permute-start | bytes 4718600 | tf_op jit(solution)/shard_map/ppermute | solution.py:123
  20.0 31.0 %copy-start.21 = (bf16[128,6,128]{2,0,1:T(8,128)(2,1)S(1)}, bf16[128,6,128]{2,0,1:T(8,128)(2,1)}, u32[]{:S(2)}) copy-start(bf16[128,6,128]{2,0,1:T(8,128)(2,1)} %copy-done.20) | copy-start | bytes 589828
  20.0 31.0 %copy-start.23 = (bf16[128,6,128]{2,0,1:T(8,128)(2,1)S(1)}, bf16[128,6,128]{2,0,1:T(8,128)(2,1)}, u32[]{:S(2)}) copy-start(bf16[128,6,128]{2,0,1:T(8,128)(2,1)} %copy-done.22) | copy-start | bytes 589828
  20.0 31.0 %copy-start.25 = (bf16[128,6,128]{2,0,1:T(8,128)(2,1)S(1)}, bf16[128,6,128]{2,0,1:T(8,128)(2,1)}, u32[]{:S(2)}) copy-start(bf16[128,6,128]{2,0,1:T(8,128)(2,1)} %copy-done.24) | copy-start | bytes 589828
  20.0 31.0 %copy-start.27 = (bf16[128,6,128]{2,0,1:T(8,128)(2,1)S(1)}, bf16[128,6,128]{2,0,1:T(8,128)(2,1)}, u32[]{:S(2)}) copy-start(bf16[128,6,128]{2,0,1:T(8,128)(2,1)} %copy-done.26) | copy-start | bytes 589828
  20.0 31.0 %copy-start.49 = (bf16[128,6,128]{2,0,1:T(8,128)(2,1)S(1)}, bf16[128,6,128]{2,0,1:T(8,128)(2,1)}, u32[]{:S(2)}) copy-start(bf16[128,6,128]{2,0,1:T(8,128)(2,1)} %copy-done.48) | copy-start | bytes 589828
  20.0 31.0 %copy-start.51 = (bf16[128,6,128]{2,0,1:T(8,128)(2,1)S(1)}, bf16[128,6,128]{2,0,1:T(8,128)(2,1)}, u32[]{:S(2)}) copy-start(bf16[128,6,128]{2,0,1:T(8,128)(2,1)} %copy-done.50) | copy-start | bytes 589828
  20.0 31.0 %copy-start.57 = (bf16[128,6,128]{2,0,1:T(8,128)(2,1)S(1)}, bf16[128,6,128]{2,0,1:T(8,128)(2,1)}, u32[]{:S(2)}) copy-start(bf16[128,6,128]{2,0,1:T(8,128)(2,1)} %copy-done.56) | copy-start | bytes 589828
  20.0 31.0 %copy-start.59 = (bf16[128,6,128]{2,0,1:T(8,128)(2,1)S(1)}, bf16[128,6,128]{2,0,1:T(8,128)(2,1)}, u32[]{:S(2)}) copy-start(bf16[128,6,128]{2,0,1:T(8,128)(2,1)} %copy-done.58) | copy-start | bytes 589828
  49.0 15.4 %collective-permute-start.2 = (bf16[2,128,12,128]{3,1,2,0:T(8,128)(2,1)S(1)}, bf16[2,128,12,128]{3,1,2,0:T(8,128)(2,1)S(1)}, u32[]{:S(2)}, u32[]{:S(2)}) collective-permute-start(bf16[2,128,12,128]{3,1,2,0:T(8,128)(2,1)S(1)} %slice.435), channel_id=1, source_target_pairs={{0,1},{1,2},{2,3},{3,4},{4,5},{5,6},{6,7},{7,8},{8,9},{9,10},{10,1... | collective-permute-start | bytes 2359304 | tf_op jit(solution)/shard_map/ppermute | solution.py:140
  69.4 11.4 %collective-permute-start.3 = (bf16[2,256,6,128]{1,3,2,0:T(8,128)(2,1)S(1)}, bf16[2,256,6,128]{1,3,2,0:T(8,128)(2,1)S(1)}, u32[]{:S(2)}, u32[]{:S(2)}) collective-permute-start(bf16[2,256,6,128]{1,3,2,0:T(8,128)(2,1)S(1)} %pad_maximum_fusion.18), channel_id=1, source_target_pairs={{1,0},{2,1},{3,2},{4,3},{5,4},{6,5},{7,6},{8,7},{9,8},{10,9},{11,1... | collective-permute-start | bytes 2359304 | tf_op jit(solution)/shard_map/ppermute | solution.py:156
  84.8 15.4 %collective-permute-start.4 = (bf16[2,256,6,128]{1,3,2,0:T(8,128)(2,1)S(1)}, bf16[2,256,6,128]{1,3,2,0:T(8,128)(2,1)S(1)}, u32[]{:S(2)}, u32[]{:S(2)}) collective-permute-start(bf16[2,256,6,128]{1,3,2,0:T(8,128)(2,1)S(1)} %pad_maximum_fusion.20), channel_id=1, source_target_pairs={{1,0},{2,1},{3,2},{4,3},{5,4},{6,5},{7,6},{8,7},{9,8},{10,9},{11,1... | collective-permute-start | bytes 2359304 | tf_op jit(solution)/shard_map/ppermute | solution.py:156
  91.9 28.5 %collective-permute-start.7 = (bf16[3,128,6,128]{1,3,2,0:T(8,128)(2,1)S(1)}, bf16[3,128,6,128]{1,3,2,0:T(8,128)(2,1)S(1)}, u32[]{:S(2)}, u32[]{:S(2)}) collective-permute-start(bf16[3,128,6,128]{1,3,2,0:T(8,128)(2,1)S(1)} %get-tuple-element.78), channel_id=1, source_target_pairs={{0,32},{32,0},{64,96},{96,64},{1,33},{33,1},{65,97},{97,65},{2,34}... | collective-permute-start | bytes 1769480 | tf_op jit(solution)/shard_map/ppermute | solution.py:166
  103.3 2.2 %copy-start.1 = (bf16[128,6,128]{2,0,1:T(8,128)(2,1)S(1)}, bf16[128,6,128]{2,0,1:T(8,128)(2,1)}, u32[]{:S(2)}) copy-start(bf16[128,6,128]{2,0,1:T(8,128)(2,1)} %copy-done) | copy-start | bytes 589828
  103.3 2.2 %copy-start.3 = (bf16[128,6,128]{2,0,1:T(8,128)(2,1)S(1)}, bf16[128,6,128]{2,0,1:T(8,128)(2,1)}, u32[]{:S(2)}) copy-start(bf16[128,6,128]{2,0,1:T(8,128)(2,1)} %copy-done.2) | copy-start | bytes 589828
  103.3 2.2 %copy-start.29 = (bf16[128,6,128]{2,0,1:T(8,128)(2,1)S(1)}, bf16[128,6,128]{2,0,1:T(8,128)(2,1)}, u32[]{:S(2)}) copy-start(bf16[128,6,128]{2,0,1:T(8,128)(2,1)} %copy-done.28) | copy-start | bytes 589828
  103.3 2.2 %copy-start.31 = (bf16[128,6,128]{2,0,1:T(8,128)(2,1)S(1)}, bf16[128,6,128]{2,0,1:T(8,128)(2,1)}, u32[]{:S(2)}) copy-start(bf16[128,6,128]{2,0,1:T(8,128)(2,1)} %copy-done.30) | copy-start | bytes 589828
  103.3 2.2 %copy-start.33 = (bf16[128,6,128]{2,0,1:T(8,128)(2,1)S(1)}, bf16[128,6,128]{2,0,1:T(8,128)(2,1)}, u32[]{:S(2)}) copy-start(bf16[128,6,128]{2,0,1:T(8,128)(2,1)} %copy-done.32) | copy-start | bytes 589828
  103.3 2.2 %copy-start.35 = (bf16[128,6,128]{2,0,1:T(8,128)(2,1)S(1)}, bf16[128,6,128]{2,0,1:T(8,128)(2,1)}, u32[]{:S(2)}) copy-start(bf16[128,6,128]{2,0,1:T(8,128)(2,1)} %copy-done.34) | copy-start | bytes 589828
  103.4 15.7 %collective-permute-start.6 = (bf16[2,128,12,128]{3,1,2,0:T(8,128)(2,1)S(1)}, bf16[2,128,12,128]{3,1,2,0:T(8,128)(2,1)S(1)}, u32[]{:S(2)}, u32[]{:S(2)}) collective-permute-start(bf16[2,128,12,128]{3,1,2,0:T(8,128)(2,1)S(1)} %slice.403), channel_id=1, source_target_pairs={{0,1},{1,2},{2,3},{3,4},{4,5},{5,6},{6,7},{7,8},{8,9},{9,10},{10,1... | collective-permute-start | bytes 2359304 | tf_op jit(solution)/shard_map/ppermute | solution.py:140
  105.8 21.9 %collective-permute-start.9 = (bf16[3,128,6,128]{1,3,2,0:T(8,128)(2,1)S(1)}, bf16[3,128,6,128]{1,3,2,0:T(8,128)(2,1)S(1)}, u32[]{:S(2)}, u32[]{:S(2)}) collective-permute-start(bf16[3,128,6,128]{1,3,2,0:T(8,128)(2,1)S(1)} %get-tuple-element.84), channel_id=1, source_target_pairs={{0,32},{32,0},{64,96},{96,64},{1,33},{33,1},{65,97},{97,65},{2,34}... | collective-permute-start | bytes 1769480 | tf_op jit(solution)/shard_map/ppermute | solution.py:166
  124.5 11.4 %collective-permute-start.8 = (bf16[2,256,6,128]{1,3,2,0:T(8,128)(2,1)S(1)}, bf16[2,256,6,128]{1,3,2,0:T(8,128)(2,1)S(1)}, u32[]{:S(2)}, u32[]{:S(2)}) collective-permute-start(bf16[2,256,6,128]{1,3,2,0:T(8,128)(2,1)S(1)} %pad_maximum_fusion.26), channel_id=1, source_target_pairs={{1,0},{2,1},{3,2},{4,3},{5,4},{6,5},{7,6},{8,7},{9,8},{10,9},{11,1... | collective-permute-start | bytes 2359304 | tf_op jit(solution)/shard_map/ppermute | solution.py:156
  140.0 15.4 %collective-permute-start.10 = (bf16[2,256,6,128]{1,3,2,0:T(8,128)(2,1)S(1)}, bf16[2,256,6,128]{1,3,2,0:T(8,128)(2,1)S(1)}, u32[]{:S(2)}, u32[]{:S(2)}) collective-permute-start(bf16[2,256,6,128]{1,3,2,0:T(8,128)(2,1)S(1)} %pad_maximum_fusion.28), channel_id=1, source_target_pairs={{1,0},{2,1},{3,2},{4,3},{5,4},{6,5},{7,6},{8,7},{9,8},{10,9},{11,1... | collective-permute-start | bytes 2359304 | tf_op jit(solution)/shard_map/ppermute | solution.py:156
  147.1 16.6 %collective-permute-start.11 = (bf16[3,128,6,128]{1,3,2,0:T(8,128)(2,1)S(1)}, bf16[3,128,6,128]{1,3,2,0:T(8,128)(2,1)S(1)}, u32[]{:S(2)}, u32[]{:S(2)}) collective-permute-start(bf16[3,128,6,128]{1,3,2,0:T(8,128)(2,1)S(1)} %get-tuple-element.80), channel_id=1, source_target_pairs={{0,32},{32,0},{64,96},{96,64},{1,33},{33,1},{65,97},{97,65},{2,34}... | collective-permute-start | bytes 1769480 | tf_op jit(solution)/shard_map/ppermute | solution.py:166
  156.6 15.2 %collective-permute-start.12 = (bf16[3,128,6,128]{1,3,2,0:T(8,128)(2,1)S(1)}, bf16[3,128,6,128]{1,3,2,0:T(8,128)(2,1)S(1)}, u32[]{:S(2)}, u32[]{:S(2)}) collective-permute-start(bf16[3,128,6,128]{1,3,2,0:T(8,128)(2,1)S(1)} %get-tuple-element.82), channel_id=1, source_target_pairs={{0,32},{32,0},{64,96},{96,64},{1,33},{33,1},{65,97},{97,65},{2,34}... | collective-permute-start | bytes 1769480 | tf_op jit(solution)/shard_map/ppermute | solution.py:166
  (28 other events, 29.2 us)
